TPU v7x, 512 devices: a whole 4x4x16 slice. The times are simulated.
512 devices in a mesh: req: 128 (over z, y, core), tp: 4 (over x).
Axes of the slice: x: 4, y: 4, z: 16, core: 2. Of those that a mesh axis runs over, the one named last changes fastest.
Arguments:
- query: bfloat16 [512, 2304], P('req', 'tp'), may hold values from -6 to 6
- new_key: bfloat16 [512, 2304], P('req', 'tp'), may hold values from -6 to 6
- new_value: bfloat16 [512, 2304], P('req', 'tp'), may hold values from -6 to 6
- key_cache: bfloat16 [512, 128, 2304], P('req', None, 'tp'), may hold values from -6 to 6
- value_cache: bfloat16 [512, 128, 2304], P('req', None, 'tp'), may hold values from -6 to 6
- lengths: int32 [512], P('req'), may hold values from 1 to 128, 32768 in all
- resid: bfloat16 [512, 2304], P('req'), may hold values from -6 to 6
- out_weight: bfloat16 [2304, 2304], P('tp'), may hold values from -0.125 to 0.125
- norm_gain: float32 [2304], P('tp'), may hold values from 0.25 to 1.75
- expert_ids: int32 [512, 2], replicated, may hold values from 0 to 7, all different within a row; in each aligned block of 4 rows (0 to 3, 4 to 7, ...) at most 2 rows name the same one
- route_weight: float32 [512, 2], replicated, may hold values from 0.2 to 1
- gate_weight: bfloat16 [2304, 46080], P('tp', 'req'), may hold values from -0.125 to 0.125
- up_weight: bfloat16 [2304, 46080], P('tp', 'req'), may hold values from -0.125 to 0.125
- down_weight: bfloat16 [46080, 2304], P('req', 'tp'), may hold values from -0.078125 to 0.078125
Outputs:
- layer_out: bfloat16 [512, 2304], P('req', 'tp')
Inputs may be any that keep to these rules, and one draw needn't show every extreme that they name: `lengths`: each request has 1 to 128 valid cached positions, and some request has exactly 128. `expert_ids`: the two experts of a token differ, every expert is chosen by some token, and in each aligned block of 4 rows (the rows of one device) no expert is chosen by more than 2 rows; in some block one expert is chosen by exactly 2 rows.
All inputs are finite; a program needn't handle non-finite values. No bound on the sum of `lengths` on one device may be relied on, other than what follows from the above.
Results may differ from a plain program's by a relative error of at most 0.007.
Values may be sent and summed in bfloat16 or wider, within the bound.
No kernel may reach another device: no remote copies, remote signals or barrier semaphores. Data moves between devices by JAX's collectives and lax.ppermute only.
A program may use at most 64 MiB of HBM per device.

v0:
```python
import jax
import jax.numpy as jnp
from jax import lax
from jax.sharding import PartitionSpec as P

HD = 64
EXPERTS = 8


def local_attention(query, new_key, new_value, key_cache, value_cache, lengths):
    row_count = query.shape[0]
    local_width = query.shape[1]
    head_count = local_width // HD
    cache_len = key_cache.shape[1]
    score_scale = HD ** (-0.5)
    queries = query.reshape(row_count, head_count, HD)
    cached_keys = key_cache.reshape(row_count, cache_len, head_count, HD)
    cached_values = value_cache.reshape(row_count, cache_len, head_count, HD)
    scores = (
        jnp.einsum("rhd,rjhd->rhj", queries, cached_keys, preferred_element_type=jnp.float32)
        * score_scale
    )
    own_score = (
        jnp.sum(
            queries.astype(jnp.float32)
            * new_key.reshape(row_count, head_count, HD).astype(jnp.float32),
            axis=-1,
        )
        * score_scale
    )
    positions = jnp.arange(cache_len, dtype=jnp.int32)
    is_valid = positions[None, None, :] < lengths[:, None, None]
    scores = jnp.where(is_valid, scores, -jnp.inf)
    highest = jnp.maximum(jnp.max(scores, axis=-1), own_score)
    cached_exp = jnp.exp(scores - highest[..., None])
    own_exp = jnp.exp(own_score - highest)
    denominator = jnp.sum(cached_exp, axis=-1) + own_exp
    cached_prob = (cached_exp / denominator[..., None]).astype(jnp.bfloat16)
    own_prob = (own_exp / denominator).astype(jnp.bfloat16)
    mixed_values = jnp.einsum(
        "rhj,rjhd->rhd", cached_prob, cached_values, preferred_element_type=jnp.float32
    )
    mixed_values = mixed_values + own_prob.astype(jnp.float32)[..., None] * new_value.reshape(
        row_count, head_count, HD
    ).astype(jnp.float32)
    return mixed_values.reshape(row_count, local_width).astype(jnp.bfloat16)


def slot_tables(block_ids, block_weights, capacity):
    blocks, rows, picks = block_ids.shape
    expert_hit = block_ids[..., None] == jnp.arange(EXPERTS, dtype=jnp.int32)
    flat_hits = expert_hit.reshape(blocks, rows * picks, EXPERTS).astype(jnp.int32)
    earlier = jnp.cumsum(flat_hits, axis=1) - flat_hits
    slot_index = jnp.sum(earlier * flat_hits, axis=-1).reshape(blocks, rows, picks)
    slot_hit = slot_index[..., None] == jnp.arange(capacity, dtype=jnp.int32)
    pair_hit = expert_hit[..., :, None] & slot_hit[..., None, :]
    selector = jnp.any(pair_hit, axis=2).astype(jnp.bfloat16)
    combiner = jnp.sum(jnp.where(pair_hit, block_weights[..., None, None], 0.0), axis=2)
    return (selector, combiner)


def shards(
    query,
    new_key,
    new_value,
    key_cache,
    value_cache,
    lengths,
    resid,
    out_weight,
    norm_gain,
    expert_ids,
    route_weight,
    gate_weight,
    up_weight,
    down_weight,
):
    row_count = query.shape[0]
    attn_out = local_attention(query, new_key, new_value, key_cache, value_cache, lengths)
    model_width = out_weight.shape[1]
    share = model_width // lax.axis_size("tp")
    col_start = lax.axis_index("tp") * share
    resid_float = resid.astype(jnp.float32)
    proj_cols = lax.psum_scatter(
        lax.dot_general(
            out_weight, attn_out, (((0,), (1,)), ((), ())), preferred_element_type=jnp.float32
        ),
        "tp",
        scatter_dimension=0,
        tiled=True,
    )
    hidden_state = lax.dynamic_slice_in_dim(resid_float, col_start, share, 1) + proj_cols.T
    square_sum = lax.psum(jnp.sum(hidden_state * hidden_state, axis=1), "tp")
    inv_rms = lax.rsqrt(square_sum / model_width + 1e-05)
    normed = (hidden_state * inv_rms[:, None] * norm_gain[None, :]).astype(jnp.bfloat16)
    req_count = lax.axis_size("req")
    group_size = req_count // EXPERTS
    capacity = max(2, row_count // 2)
    first_row = lax.axis_index("req") * row_count
    my_ids = lax.dynamic_slice_in_dim(expert_ids, first_row, row_count, 0)
    my_weights = lax.dynamic_slice_in_dim(route_weight, first_row, row_count, 0)
    selector, combiner = slot_tables(my_ids[None], my_weights[None], capacity)
    expert_rows = jnp.einsum(
        "tec,tf->ecf", selector[0], normed, preferred_element_type=jnp.float32
    ).astype(jnp.bfloat16)
    outgoing = jnp.repeat(expert_rows, group_size, axis=0)
    arrived = lax.all_to_all(outgoing, "req", split_axis=0, concat_axis=0, tiled=True)
    token_rows = arrived.reshape(req_count * capacity, share)
    gate_part = jnp.dot(token_rows, gate_weight, preferred_element_type=jnp.float32)
    up_part = jnp.dot(token_rows, up_weight, preferred_element_type=jnp.float32)
    gate_part, up_part = lax.psum((gate_part, up_part), "tp")
    activ = (jax.nn.silu(gate_part) * up_part).astype(jnp.bfloat16)
    partial_out = jnp.dot(activ, down_weight, preferred_element_type=jnp.float32).reshape(
        req_count, capacity, share
    )
    returned = lax.all_to_all(partial_out, "req", split_axis=0, concat_axis=0, tiled=True)
    grouped = jnp.sum(returned.reshape(EXPERTS, group_size, capacity, share), axis=1)
    moe_sum = jnp.einsum("tec,ecf->tf", combiner[0], grouped, precision=lax.Precision.HIGHEST)
    return (hidden_state + moe_sum).astype(jnp.bfloat16)


def solution(mesh):
    placed = (
        P("req", "tp"),
        P("req", "tp"),
        P("req", "tp"),
        P("req", None, "tp"),
        P("req", None, "tp"),
        P("req"),
        P("req", None),
        P("tp", None),
        P("tp"),
        P(),
        P(),
        P("tp", "req"),
        P("tp", "req"),
        P("req", "tp"),
    )
    return jax.shard_map(
        shards, mesh=mesh, in_specs=placed, out_specs=P("req", "tp"), check_vma=False
    )
```

profile of v0, /device:TPU:33, one launch (start us, length us, event | category | flops | bytes accessed | tf_op | source)
XLA Modules:
  0.0 224.8 jit_solution(13222458131651996288)
XLA Ops:
  6.5 0.9 reshape.231
  7.5 0.8 reshape.215
  8.2 0.7 iota_compare_fusion.3
  9.0 1.3 fusion.21
  10.3 0.1 fusion.16
  10.4 0.1 copy.43
  10.5 0.8 reshape.222
  11.3 0.1 multiply_reduce_fusion
  11.4 0.1 copy.44
  11.5 0.2 fusion.9
  11.6 0.1 copy.45
  11.7 0.1 copy.46
  11.8 0.1 fusion.10
  11.9 0.8 reshape.223
  12.7 1.5 fusion.7
  14.2 0.1 fusion.5
  14.2 0.1 convert_element_type.79
  14.4 0.5 convolution_bitcast_fusion
  14.8 1.4 copy.57
  16.3 0.0 all-reduce.3.cloned.1.call-start
  16.3 0.8 constant_dynamic-slice_fusion.1
  17.1 0.1 copy.47
  17.2 0.1 iota_compare_fusion.1
  17.3 0.1 eq.65
  17.3 0.1 fusion.17
  17.4 0.2 select_reduce_fusion
  17.6 0.1 eq.69
  17.7 0.1 copy.48
  17.8 33.3 %reduce-scatter.4.cloned.1.call-done = f32[576,4]{1,0:T(8,128)} async-done(((f32[2304,4]{1,0:T(8,128)}), f32[576,4]{1,0:T(8,128)}) %reduce-scatter.4.cloned.1.call-update) | async-done | bytes 9232
  51.1 1.1 copy.58
  52.2 0.2 multiply_reduce_fusion.1
  52.4 0.1 and_reduce_fusion
  52.5 6.8 %psum.21 = f32[4]{0:T(128)S(1)} all-reduce(f32[4]{0:T(128)S(1)} %multiply_reduce_fusion.1), channel_id=1, replica_groups=mesh['req'=128,'tp'=4] {'tp'}, use_global_device_ids=true, to_apply=%region_9.10 | all-reduce | flops 4 | bytes 32 | tf_op jit(solution)/shard_map/psum | solution.py:93
  59.3 0.2 convolution_convert_fusion
  59.5 0.2 broadcast_in_dim.42
  59.7 44.8 %all_to_all.10 = bf16[128,2,576]{2,1,0:T(2,128)(2,1)S(1)} all-to-all(bf16[128,2,576]{2,1,0:T(2,128)(2,1)S(1)} %bitcast.54), channel_id=1, replica_groups=mesh['req'=128,'tp'=4] {'req'}, dimensions={0} | all-to-all | bytes 589824 | tf_op jit(solution)/shard_map/all_to_all | solution.py:107
  104.5 0.2 reshape.219
  104.8 2.1 fusion.22
  106.9 2.1 fusion.23
  109.1 46.7 %all-reduce.3.cloned.1.call-done = (f32[256,360]{0,1:T(8,128)}, f32[256,360]{0,1:T(8,128)}) async-done(((f32[256,360]{0,1:T(8,128)}, f32[256,360]{0,1:T(8,128)}), (f32[256,360]{0,1:T(8,128)}, f32[256,360]{0,1:T(8,128)})) %all-reduce.3.cloned.1.call-update) | async-done | bytes 737296 | tf_op jit(solution)/shard_map/psum | solution.py:111
  155.8 1.7 fusion.2
  157.4 1.2 reshape.220
  158.7 19.1 %all-to-all-start.1 = ((f32[128,2,576]{2,1,0:T(2,128)}), f32[128,2,576]{2,1,0:T(2,128)S(1)}, u32[]{:S(2)}, u32[]{:S(2)}) async-start(f32[128,2,576]{2,1,0:T(2,128)} %reshape.220), calls=%async_computation.1 | async-start | bytes 1310720 | tf_op jit(solution)/shard_map/all_to_all | solution.py:116
  177.8 0.8 constant_dynamic-slice_fusion
  178.6 0.1 fusion.11
  178.7 38.3 %all-to-all-done.1 = f32[128,2,576]{2,1,0:T(2,128)S(1)} async-done(((f32[128,2,576]{2,1,0:T(2,128)}), f32[128,2,576]{2,1,0:T(2,128)S(1)}, u32[]{:S(2)}, u32[]{:S(2)}) %all-to-all-start.1) | async-done | bytes 589856 | tf_op jit(solution)/shard_map/all_to_all | solution.py:116
  216.9 0.1 bitcast_reduce_fusion
  217.1 0.8 fusion.1
  (15 shorter events, 0.1 us)
Async XLA Ops:
  6.5 7.8 %copy-start = (bf16[576,2304]{1,0:T(8,128)(2,1)S(1)}, bf16[576,2304]{1,0:T(8,128)(2,1)}, u32[]{:S(2)}) copy-start(bf16[576,2304]{1,0:T(8,128)(2,1)} %param.21) | copy-start | bytes 7962628
  6.5 44.6 %reduce-scatter.4.cloned.1.call-start = ((), (), s32[]{:S(2)}) async-start(), calls=%async_computation.3 | async-start | bytes 1474560
  14.4 37.8 %copy-start.1 = (bf16[4,2304]{1,0:T(4,128)(2,1)S(1)}, bf16[4,2304]{1,0:T(4,128)(2,1)}, u32[]{:S(2)}) copy-start(bf16[4,2304]{1,0:T(4,128)(2,1)} %param.20) | copy-start | bytes 55300
  14.4 44.9 %copy-start.2 = (f32[576]{0:T(1024)S(1)}, f32[576]{0:T(1024)}, u32[]{:S(2)}) copy-start(f32[576]{0:T(1024)} %param.22) | copy-start | bytes 6916
  16.3 139.5 %all-reduce.3.cloned.1.call-start = ((), (), s32[]{:S(2)}) async-start(), calls=%async_computation.4 | async-start | bytes 1474560 | tf_op jit(solution)/shard_map/psum | solution.py:111
  158.7 58.3 %all-to-all-start.1 = ((f32[128,2,576]{2,1,0:T(2,128)}), f32[128,2,576]{2,1,0:T(2,128)S(1)}, u32[]{:S(2)}, u32[]{:S(2)}) async-start(f32[128,2,576]{2,1,0:T(2,128)} %reshape.220), calls=%async_computation.1 | async-start | bytes 1310720 | tf_op jit(solution)/shard_map/all_to_all | solution.py:116
Sparse Core Ops, SparseCore 0:
  16.4 34.6 reduce-scatter.3
  109.2 46.5 all-reduce.2
where the time goes:
time: 225 us
  waiting for transfers between devices  118 us (52%)
  blocking collectives  51.6 us (23%)
  starting transfers between devices  19.2 us (9%)
  between operations  13.5 us (6%)
  matrix products  10.2 us (5%)
  local copies, waits for them, and re-layouts  9.8 us (4%)
    psum x1, waiting for transfers between devices, shards(): gate_part, up_part = lax.psum((gate_part, up_part), 'tp')  46.7 us
    all_to_all x1, blocking collectives, shards(): lax.all_to_all(outgoing, 'req', split_axis=0, concat_axis=0, tiled=True)  44.8 us
    all_to_all x1, waiting for transfers between devices, shards(): lax.all_to_all(partial_out, 'req', split_axis=0, concat_axis=0, tiled=True)  38.3 us
    unnamed x3, waiting for transfers between devices  33.3 us
    all_to_all x1, starting transfers between devices, shards(): lax.all_to_all(partial_out, 'req', split_axis=0, concat_axis=0, tiled=True)  19.1 us
    psum x1, blocking collectives, shards(): square_sum = lax.psum(jnp.sum(hidden_state * hidden_state, axis=1), 'tp')  6.77 us
  transfers between devices with their start and end apart: 3, of which 3 were waited for; matrix products, arithmetic and copies ran while one was open for 1% of the time, Pallas kernels for 0%

commit v1 on v0

--- a/solution.py
+++ b/solution.py
@@ -81,17 +81,12 @@
     share = model_width // lax.axis_size("tp")
     col_start = lax.axis_index("tp") * share
     resid_float = resid.astype(jnp.float32)
-    proj_cols = lax.psum_scatter(
-        lax.dot_general(
-            out_weight, attn_out, (((0,), (1,)), ((), ())), preferred_element_type=jnp.float32
-        ),
-        "tp",
-        scatter_dimension=0,
-        tiled=True,
-    )
-    hidden_state = lax.dynamic_slice_in_dim(resid_float, col_start, share, 1) + proj_cols.T
-    square_sum = lax.psum(jnp.sum(hidden_state * hidden_state, axis=1), "tp")
-    inv_rms = lax.rsqrt(square_sum / model_width + 1e-05)
+    proj_part = jnp.dot(attn_out, out_weight, preferred_element_type=jnp.float32)
+    proj_all = lax.all_gather(proj_part, "tp", axis=0, tiled=False)
+    hidden_full = resid_float + jnp.sum(proj_all, axis=0)
+    mean_square = jnp.mean(hidden_full * hidden_full, axis=1)
+    inv_rms = lax.rsqrt(mean_square + 1e-05)
+    hidden_state = lax.dynamic_slice_in_dim(hidden_full, col_start, share, 1)
     normed = (hidden_state * inv_rms[:, None] * norm_gain[None, :]).astype(jnp.bfloat16)
     req_count = lax.axis_size("req")
     group_size = req_count // EXPERTS
@@ -110,11 +105,15 @@
     up_part = jnp.dot(token_rows, up_weight, preferred_element_type=jnp.float32)
     gate_part, up_part = lax.psum((gate_part, up_part), "tp")
     activ = (jax.nn.silu(gate_part) * up_part).astype(jnp.bfloat16)
-    partial_out = jnp.dot(activ, down_weight, preferred_element_type=jnp.float32).reshape(
-        req_count, capacity, share
+    partial_out = (
+        jnp.dot(activ, down_weight, preferred_element_type=jnp.float32)
+        .astype(jnp.bfloat16)
+        .reshape(req_count, capacity, share)
     )
     returned = lax.all_to_all(partial_out, "req", split_axis=0, concat_axis=0, tiled=True)
-    grouped = jnp.sum(returned.reshape(EXPERTS, group_size, capacity, share), axis=1)
+    grouped = jnp.sum(
+        returned.reshape(EXPERTS, group_size, capacity, share).astype(jnp.float32), axis=1
+    )
     moe_sum = jnp.einsum("tec,ecf->tf", combiner[0], grouped, precision=lax.Precision.HIGHEST)
     return (hidden_state + moe_sum).astype(jnp.bfloat16)
 

time: 225 us -> 182 us (0.81)
  waiting for transfers between devices: 118 us -> 72.4 us
  blocking collectives: 51.6 us -> 57.1 us
  local copies, waits for them, and re-layouts: 9.8 us -> 7.11 us
    unnamed x3 -> x1, waiting for transfers between devices: 33.3 us -> 0.02 us
    all_to_all x1, waiting for transfers between devices: 38.3 us -> 24.6 us  [shards(): lax.all_to_all(partial_out, 'req', split_axis=0, concat_axis=0, tiled=True)]
    all_gather x0 -> x1, blocking collectives: none -> 9.52 us  [shards(): proj_all = lax.all_gather(proj_part, 'tp', axis=0, tiled=False)]
    psum x1 -> x0, blocking collectives: 6.77 us -> none  [shards(): square_sum = lax.psum(jnp.sum(hidden_state * hidden_state, axis=1), 'tp')]
    all_to_all x1, blocking collectives: 44.8 us -> 47.5 us  [shards(): lax.all_to_all(outgoing, 'req', split_axis=0, concat_axis=0, tiled=True)]
    unnamed x8 -> x6, local copies, waits for them, and re-layouts: 2.52 us -> 0.01 us
  transfers between devices with their start and end apart: 3 -> 2, of which waited for: 3 -> 2; matrix products, arithmetic and copies ran while one was open for 1% -> 0% of each run, Pallas kernels for 0% -> 0%
where the time goes in v1:
time: 182 us
  waiting for transfers between devices  72.4 us (40%)
  blocking collectives  57.1 us (31%)
  starting transfers between devices  19.1 us (10%)
  between operations  13.5 us (7%)
  matrix products  10.2 us (6%)
  local copies, waits for them, and re-layouts  7.11 us (4%)
  other arithmetic  2.28 us (1%)
    psum x1, waiting for transfers between devices, shards(): gate_part, up_part = lax.psum((gate_part, up_part), 'tp')  47.8 us
    all_to_all x1, blocking collectives, shards(): lax.all_to_all(outgoing, 'req', split_axis=0, concat_axis=0, tiled=True)  47.5 us
    all_to_all x1, waiting for transfers between devices, shards(): lax.all_to_all(partial_out, 'req', split_axis=0, concat_axis=0, tiled=True)  24.6 us
    all_to_all x1, starting transfers between devices, shards(): lax.all_to_all(partial_out, 'req', split_axis=0, concat_axis=0, tiled=True)  19.1 us
    all_gather x1, blocking collectives, shards(): proj_all = lax.all_gather(proj_part, 'tp', axis=0, tiled=False)  9.52 us
  transfers between devices with their start and end apart: 2, of which 2 were waited for; matrix products, arithmetic and copies ran while one was open for 0% of the time, Pallas kernels for 0%

profile of v1, /device:TPU:33, one launch (start us, length us, event | category | flops | bytes accessed | tf_op | source)
XLA Modules:
  0.0 181.7 jit_solution(15906947744491657381)
XLA Ops:
  6.5 0.0 copy-start
  6.5 0.9 reshape.239
  7.5 0.8 reshape.219
  8.3 0.7 constant_dynamic-slice_fusion.1
  9.0 0.1 copy.47
  9.1 0.1 iota_compare_fusion.1
  9.2 0.7 iota_compare_fusion.3
  9.9 1.3 fusion.21
  11.2 0.1 fusion.15
  11.3 0.1 copy.43
  11.4 0.8 reshape.225
  12.2 0.1 multiply_reduce_fusion.1
  12.3 0.1 copy.44
  12.4 0.2 fusion.8
  12.6 0.1 copy.45
  12.7 0.1 copy.46
  12.8 0.1 fusion.9
  12.9 0.8 reshape.226
  13.6 1.5 fusion.6
  15.1 0.1 fusion.4
  15.2 0.1 convert_element_type.88
  15.3 0.5 convolution_bitcast_fusion
  15.8 9.5 %all-gather.1 = f32[4,4,2304]{2,1,0:T(4,128)S(1)} all-gather(f32[1,4,2304]{2,1,0:T(4,128)S(1)} %convolution_bitcast_fusion), channel_id=2, replica_groups=mesh['req'=128,'tp'=4] {'tp'}, dimensions={0}, use_global_device_ids=true | all-gather | bytes 184320 | tf_op jit(solution)/shard_map/all_gather | solution.py:85
  25.3 0.0 copy-done.1
  25.3 0.1 multiply_reduce_fusion
  25.5 0.1 eq.65
  25.5 0.1 fusion.16
  25.6 0.2 select_reduce_fusion
  25.8 0.1 eq.69
  25.9 0.1 copy.48
  26.0 0.1 and_reduce_fusion
  26.1 0.2 convolution_convert_fusion.1
  26.4 0.2 broadcast_in_dim.42
  26.6 47.5 %all_to_all.10 = bf16[128,2,576]{2,1,0:T(2,128)(2,1)S(1)} all-to-all(bf16[128,2,576]{2,1,0:T(2,128)(2,1)S(1)} %bitcast.45), channel_id=1, replica_groups=mesh['req'=128,'tp'=4] {'req'}, dimensions={0} | all-to-all | bytes 589824 | tf_op jit(solution)/shard_map/all_to_all | solution.py:102
  74.1 0.2 reshape.223
  74.4 2.1 %fusion.22 = f32[256,360]{0,1:T(8,128)} fusion(bf16[256,576]{1,0:T(8,128)(2,1)S(1)} %reshape.223, bf16[576,360]{1,0:T(8,128)(2,1)} %param.25), kind=kOutput, calls=%fused_computation.48 | convolution fusion | flops 106168320 | bytes 1078272 | tf_op jit(solution)/shard_map/dot_general | solution.py:104
  76.5 2.1 %fusion.23 = f32[256,360]{0,1:T(8,128)} fusion(bf16[256,576]{1,0:T(8,128)(2,1)S(1)} %reshape.223, bf16[576,360]{1,0:T(8,128)(2,1)} %param.26), kind=kOutput, calls=%fused_computation.49 | convolution fusion | flops 106168320 | bytes 1078272 | tf_op jit(solution)/shard_map/dot_general | solution.py:105
  78.6 0.0 all-reduce.3.cloned.1.call-update
  78.7 47.8 %all-reduce.3.cloned.1.call-done = (f32[256,360]{0,1:T(8,128)}, f32[256,360]{0,1:T(8,128)}) async-done(((f32[256,360]{0,1:T(8,128)}, f32[256,360]{0,1:T(8,128)}), (f32[256,360]{0,1:T(8,128)}, f32[256,360]{0,1:T(8,128)})) %all-reduce.3.cloned.1.call-update) | async-done | bytes 737296 | tf_op jit(solution)/shard_map/psum | solution.py:106
  126.5 1.6 convolution_convert_fusion
  128.1 0.2 copy.50
  128.3 0.9 reshape.224
  129.2 19.1 %all-to-all-start.1 = ((bf16[128,2,576]{2,1,0:T(2,128)(2,1)}), bf16[128,2,576]{2,1,0:T(2,128)(2,1)S(1)}, u32[]{:S(2)}, u32[]{:S(2)}) async-start(bf16[128,2,576]{2,1,0:T(2,128)(2,1)} %reshape.224), calls=%async_computation.1 | async-start | bytes 655360 | tf_op jit(solution)/shard_map/all_to_all | solution.py:113
  148.3 0.8 constant_dynamic-slice_fusion
  149.1 0.1 fusion.10
  149.2 24.6 %all-to-all-done.1 = bf16[128,2,576]{2,1,0:T(2,128)(2,1)S(1)} async-done(((bf16[128,2,576]{2,1,0:T(2,128)(2,1)}), bf16[128,2,576]{2,1,0:T(2,128)(2,1)S(1)}, u32[]{:S(2)}, u32[]{:S(2)}) %all-to-all-start.1) | async-done | bytes 294944 | tf_op jit(solution)/shard_map/all_to_all | solution.py:113
  173.7 0.3 convert_reduce_fusion
  174.0 0.8 fusion.1
  (12 shorter events, 0.1 us)
Async XLA Ops:
  6.5 8.8 %copy-start = (bf16[576,2304]{1,0:T(8,128)(2,1)S(1)}, bf16[576,2304]{1,0:T(8,128)(2,1)}, u32[]{:S(2)}) copy-start(bf16[576,2304]{1,0:T(8,128)(2,1)} %param.21) | copy-start | bytes 7962628
  6.5 18.8 %copy-start.1 = (bf16[4,2304]{1,0:T(4,128)(2,1)S(1)}, bf16[4,2304]{1,0:T(4,128)(2,1)}, u32[]{:S(2)}) copy-start(bf16[4,2304]{1,0:T(4,128)(2,1)} %param.20) | copy-start | bytes 55300
  6.5 19.6 %copy-start.2 = (f32[576]{0:T(1024)S(1)}, f32[576]{0:T(1024)}, u32[]{:S(2)}) copy-start(f32[576]{0:T(1024)} %param.22) | copy-start | bytes 6916
  6.5 119.9 %all-reduce.3.cloned.1.call-start = ((), (), s32[]{:S(2)}) async-start(), calls=%async_computation.2 | async-start | bytes 1474560 | tf_op jit(solution)/shard_map/psum | solution.py:106
  129.2 44.5 %all-to-all-start.1 = ((bf16[128,2,576]{2,1,0:T(2,128)(2,1)}), bf16[128,2,576]{2,1,0:T(2,128)(2,1)S(1)}, u32[]{:S(2)}, u32[]{:S(2)}) async-start(bf16[128,2,576]{2,1,0:T(2,128)(2,1)} %reshape.224), calls=%async_computation.1 | async-start | bytes 655360 | tf_op jit(solution)/shard_map/all_to_all | solution.py:113
Sparse Core Ops, SparseCore 0:
  78.8 47.6 all-reduce.2

commit v2 on v1

--- a/solution.py
+++ b/solution.py
@@ -103,8 +103,18 @@
     token_rows = arrived.reshape(req_count * capacity, share)
     gate_part = jnp.dot(token_rows, gate_weight, preferred_element_type=jnp.float32)
     up_part = jnp.dot(token_rows, up_weight, preferred_element_type=jnp.float32)
-    gate_part, up_part = lax.psum((gate_part, up_part), "tp")
-    activ = (jax.nn.silu(gate_part) * up_part).astype(jnp.bfloat16)
+    tp_count = lax.axis_size("tp")
+    slot_count = token_rows.shape[0]
+    chunk = gate_part.shape[1] // tp_count
+    both = jnp.stack(
+        [gate_part.reshape(slot_count, tp_count, chunk), up_part.reshape(slot_count, tp_count, chunk)],
+        axis=2,
+    )
+    both = jnp.moveaxis(both, 1, 0).astype(jnp.bfloat16)
+    both = lax.all_to_all(both, "tp", split_axis=0, concat_axis=0, tiled=True)
+    summed = jnp.sum(both.astype(jnp.float32), axis=0)
+    activ_chunk = (jax.nn.silu(summed[:, 0]) * summed[:, 1]).astype(jnp.bfloat16)
+    activ = lax.all_gather(activ_chunk, "tp", axis=1, tiled=True)
     partial_out = (
         jnp.dot(activ, down_weight, preferred_element_type=jnp.float32)
         .astype(jnp.bfloat16)

time: 182 us -> 132 us (0.73)
  waiting for transfers between devices: 72.4 us -> 43.6 us
  blocking collectives: 57.1 us -> 29.5 us
  between operations: 13.5 us -> 0.19 us
  starting transfers between devices: 19.1 us -> 32.2 us
  local copies, waits for them, and re-layouts: 7.11 us -> 15.5 us
  matrix products: 10.2 us -> 7.33 us
    psum x1 -> x0, waiting for transfers between devices: 47.8 us -> none  [shards(): gate_part, up_part = lax.psum((gate_part, up_part), 'tp')]
    all_to_all x1, blocking collectives: 47.5 us -> 10.8 us  [shards(): both = lax.all_to_all(both, 'tp', split_axis=0, concat_axis=0, tiled=True)]
    all_to_all x0 -> x1, starting transfers between devices: none -> 22.7 us  [shards(): lax.all_to_all(outgoing, 'req', split_axis=0, concat_axis=0, tiled=True)]
    all_to_all x0 -> x1, waiting for transfers between devices: none -> 19 us  [shards(): lax.all_to_all(outgoing, 'req', split_axis=0, concat_axis=0, tiled=True)]
    all_to_all x1, starting transfers between devices: 19.1 us -> 9.47 us  [shards(): lax.all_to_all(partial_out, 'req', split_axis=0, concat_axis=0, tiled=True)]
    all_gather x0 -> x1, blocking collectives: none -> 9.25 us  [shards(): activ = lax.all_gather(activ_chunk, 'tp', axis=1, tiled=True)]
    another operation x0 -> x2, local copies, waits for them, and re-layouts: none -> 3.08 us
    dot_general x0 -> x2, local copies, waits for them, and re-layouts: none -> 3 us  [the longest x1 2 us: shards(): up_part = jnp.dot(token_rows, up_weight, preferred_element_type=jnp.float32)]
  transfers between devices with their start and end apart: 2 -> 2, of which waited for: 2 -> 2; matrix products, arithmetic and copies ran while one was open for 0% -> 5% of each run, Pallas kernels for 0% -> 0%
where the time goes in v2:
time: 132 us; the launch traced here: 131 us
  waiting for transfers between devices  43.6 us (33%)
  starting transfers between devices  32.2 us (24%)
  blocking collectives  29.5 us (22%)
  local copies, waits for them, and re-layouts  15.5 us (12%)
  matrix products  7.33 us (6%)
  other arithmetic  2.7 us (2%)
    all_to_all x1, waiting for transfers between devices, shards(): lax.all_to_all(partial_out, 'req', split_axis=0, concat_axis=0, tiled=True)  24.6 us
    all_to_all x1, starting transfers between devices, shards(): lax.all_to_all(outgoing, 'req', split_axis=0, concat_axis=0, tiled=True)  22.7 us
    all_to_all x1, waiting for transfers between devices, shards(): lax.all_to_all(outgoing, 'req', split_axis=0, concat_axis=0, tiled=True)  19 us
    all_to_all x1, blocking collectives, shards(): both = lax.all_to_all(both, 'tp', split_axis=0, concat_axis=0, tiled=True)  10.8 us
    all_gather x1, blocking collectives, shards(): proj_all = lax.all_gather(proj_part, 'tp', axis=0, tiled=False)  9.52 us
    all_to_all x1, starting transfers between devices, shards(): lax.all_to_all(partial_out, 'req', split_axis=0, concat_axis=0, tiled=True)  9.47 us
    all_gather x1, blocking collectives, shards(): activ = lax.all_gather(activ_chunk, 'tp', axis=1, tiled=True)  9.25 us
    another operation x2, local copies, waits for them, and re-layouts  3.08 us
  transfers between devices with their start and end apart: 2, of which 2 were waited for; matrix products, arithmetic and copies ran while one was open for 5% of the time, Pallas kernels for 0%

profile of v2, /device:TPU:33, one launch (start us, length us, event | category | flops | bytes accessed | tf_op | source)
XLA Modules:
  0.0 131.0 jit_solution(14203969618633530671)
XLA Ops:
  0.0 0.9 reshape.259
  0.9 0.8 reshape.233
  1.7 0.7 constant_dynamic-slice_fusion.1
  2.5 0.1 copy.83
  2.6 0.7 iota_compare_fusion.3
  3.4 1.3 %fusion.26 = f32[4,9,1,128]{3,2,1,0:T(1,128)S(1)} fusion(bf16[4,9,64,1]{2,3,1,0:T(2,128)(2,1)S(1)} %reshape.259, bf16[4,128,9,64]{1,3,2,0:T(8,128)(2,1)} %bitcast.76), kind=kOutput, calls=%fused_computation.57 | convolution fusion | flops 589824 | bytes 612864 | tf_op jit(solution)/shard_map/rhd,rjhd->rhj/dot_general | solution.py:20
  4.7 0.1 fusion.20
  4.8 0.1 copy.79
  4.9 0.8 reshape.241
  5.7 0.1 multiply_reduce_fusion.1
  5.8 0.1 copy.80
  5.9 0.2 fusion.13
  6.1 0.1 copy.81
  6.2 0.1 copy.82
  6.3 0.1 fusion.14
  6.4 0.8 reshape.242
  7.1 1.5 %fusion.11 = f32[4,9,1,64]{3,2,1,0:T(1,128)S(1)} fusion(bf16[4,128,9,64]{1,3,2,0:T(8,128)(2,1)} %bitcast.77, bf16[4,9,128,1]{2,0,1,3:T(4,128)(2,1)S(1)} %fusion.14), kind=kOutput, calls=%fused_computation.27 | convolution fusion | flops 589824 | bytes 608256 | tf_op jit(solution)/shard_map/rhj,rjhd->rhd/dot_general | solution.py:40
  8.7 0.1 convert_element_type.95
  8.8 0.5 convolution_bitcast_fusion
  9.3 9.5 %all-gather.1 = f32[4,4,2304]{2,1,0:T(4,128)S(1)} all-gather(f32[1,4,2304]{2,1,0:T(4,128)S(1)} %convolution_bitcast_fusion), channel_id=2, replica_groups=mesh['req'=128,'tp'=4] {'tp'}, dimensions={0}, use_global_device_ids=true | all-gather | bytes 184320 | tf_op jit(solution)/shard_map/all_gather | solution.py:85
  18.8 0.1 multiply_reduce_fusion
  19.2 0.2 select_reduce_fusion
  19.4 0.1 copy.84
  19.5 0.1 and_reduce_fusion
  19.6 0.2 convolution_convert_fusion.3
  19.9 0.9 broadcast_in_dim.42
  20.8 22.7 %all-to-all-start = ((bf16[128,2,576]{2,1,0:T(2,128)(2,1)}), bf16[128,2,576]{2,1,0:T(2,128)(2,1)}, u32[]{:S(2)}, u32[]{:S(2)}) async-start(bf16[128,2,576]{2,1,0:T(2,128)(2,1)} %bitcast.7), calls=%async_computation | async-start | bytes 655360 | tf_op jit(solution)/shard_map/all_to_all | solution.py:102
  43.5 1.0 copy.86
  44.5 1.1 reshape.238
  45.7 2.0 %copy.88 = bf16[360,576]{1,0:T(8,128)(2,1)} copy(bf16[360,576]{0,1:T(8,128)(2,1)} %bitcast.75) | data formatting | bytes 829440 | tf_op jit(solution)/shard_map/dot_general | solution.py:105
  47.7 1.9 %reshape.239 = bf16[4,90,576]{2,1,0:T(8,128)(2,1)} reshape(bf16[360,576]{1,0:T(8,128)(2,1)} %copy.88) | data formatting | bytes 829440 | tf_op jit(solution)/shard_map/reshape.101
  49.6 19.0 %all-to-all-done = bf16[128,2,576]{2,1,0:T(2,128)(2,1)} async-done(((bf16[128,2,576]{2,1,0:T(2,128)(2,1)}), bf16[128,2,576]{2,1,0:T(2,128)(2,1)}, u32[]{:S(2)}, u32[]{:S(2)}) %all-to-all-start) | async-done | bytes 294944 | tf_op jit(solution)/shard_map/all_to_all | solution.py:102
  68.6 1.2 reshape.237
  69.9 0.3 fusion
  70.2 1.4 %fusion.1 = bf16[256,4,1,90]{0,3,1,2:T(8,128)(2,1)S(1)} fusion(bf16[4,90,576]{2,1,0:T(8,128)(2,1)} %reshape.239, bf16[256,576]{1,0:T(8,128)(2,1)S(1)} %reshape.237), kind=kOutput, calls=%fused_computation.5 | convolution fusion | flops 106260480 | bytes 893952 | tf_op jit(solution)/shard_map/dot_general | solution.py:105
  71.7 0.4 copy.90
  72.0 10.8 %all_to_all.15 = bf16[4,256,2,90]{1,2,3,0:T(2,128)(2,1)S(1)} all-to-all(bf16[4,256,2,90]{1,2,3,0:T(2,128)(2,1)S(1)} %copy.90), channel_id=1, replica_groups=mesh['req'=128,'tp'=4] {'tp'}, dimensions={0} | all-to-all | bytes 737280 | tf_op jit(solution)/shard_map/all_to_all | solution.py:114
  82.8 0.3 convert_reduce_fusion
  83.2 0.1 fusion.25
  83.4 9.2 %all-gather.2 = bf16[4,90,256]{2,1,0:T(8,128)(2,1)S(1)} all-gather(bf16[1,90,256]{2,1,0:T(8,128)(2,1)S(1)} %fusion.7), channel_id=1, replica_groups=mesh['req'=128,'tp'=4] {'tp'}, dimensions={0}, use_global_device_ids=true | all-gather | bytes 230400 | tf_op jit(solution)/shard_map/all_gather | solution.py:117
  92.7 1.3 %convolution_convert_fusion = bf16[256,576]{0,1:T(8,128)(2,1)S(1)} fusion(bf16[360,256]{1,0:T(8,128)(2,1)S(1)} %reshape.248, bf16[360,576]{0,1:T(8,128)(2,1)} %param.27), kind=kOutput, calls=%fused_computation.1 | convolution fusion | flops 106315776 | bytes 893952 | tf_op jit(solution)/shard_map/dot_general | solution.py:119
  94.0 0.2 copy.92
  94.2 0.9 reshape.240
  95.0 9.5 %all-to-all-start.2 = ((bf16[128,2,576]{2,1,0:T(2,128)(2,1)}), bf16[128,2,576]{2,1,0:T(2,128)(2,1)S(1)}, u32[]{:S(2)}, u32[]{:S(2)}) async-start(bf16[128,2,576]{2,1,0:T(2,128)(2,1)} %reshape.240), calls=%async_computation.2 | async-start | bytes 655360 | tf_op jit(solution)/shard_map/all_to_all | solution.py:123
  104.5 0.8 constant_dynamic-slice_fusion
  105.4 24.6 %all-to-all-done.2 = bf16[128,2,576]{2,1,0:T(2,128)(2,1)S(1)} async-done(((bf16[128,2,576]{2,1,0:T(2,128)(2,1)}), bf16[128,2,576]{2,1,0:T(2,128)(2,1)S(1)}, u32[]{:S(2)}, u32[]{:S(2)}) %all-to-all-start.2) | async-done | bytes 294944 | tf_op jit(solution)/shard_map/all_to_all | solution.py:123
  129.9 0.3 convert_reduce_fusion.1
  130.2 0.8 fusion.3
  (24 shorter events, 0.7 us)
Async XLA Ops:
  0.0 8.8 %copy-start = (bf16[576,2304]{1,0:T(8,128)(2,1)S(1)}, bf16[576,2304]{1,0:T(8,128)(2,1)}, u32[]{:S(2)}) copy-start(bf16[576,2304]{1,0:T(8,128)(2,1)} %param.21) | copy-start | bytes 7962628
  0.0 18.8 %copy-start.2 = (bf16[4,2304]{1,0:T(4,128)(2,1)S(1)}, bf16[4,2304]{1,0:T(4,128)(2,1)}, u32[]{:S(2)}) copy-start(bf16[4,2304]{1,0:T(4,128)(2,1)} %param.20) | copy-start | bytes 55300
  0.0 19.6 %copy-start.3 = (f32[576]{0:T(1024)S(1)}, f32[576]{0:T(1024)}, u32[]{:S(2)}) copy-start(f32[576]{0:T(1024)} %param.22) | copy-start | bytes 6916
  4.8 38.7 %copy-start.1 = (bf16[576,360]{1,0:T(8,128)(2,1)S(1)}, bf16[576,360]{1,0:T(8,128)(2,1)}, u32[]{:S(2)}) copy-start(bf16[576,360]{1,0:T(8,128)(2,1)} %param.25) | copy-start | bytes 1244164
  20.8 47.9 %all-to-all-start = ((bf16[128,2,576]{2,1,0:T(2,128)(2,1)}), bf16[128,2,576]{2,1,0:T(2,128)(2,1)}, u32[]{:S(2)}, u32[]{:S(2)}) async-start(bf16[128,2,576]{2,1,0:T(2,128)(2,1)} %bitcast.7), calls=%async_computation | async-start | bytes 655360 | tf_op jit(solution)/shard_map/all_to_all | solution.py:102
  95.0 34.9 %all-to-all-start.2 = ((bf16[128,2,576]{2,1,0:T(2,128)(2,1)}), bf16[128,2,576]{2,1,0:T(2,128)(2,1)S(1)}, u32[]{:S(2)}, u32[]{:S(2)}) async-start(bf16[128,2,576]{2,1,0:T(2,128)(2,1)} %reshape.240), calls=%async_computation.2 | async-start | bytes 655360 | tf_op jit(solution)/shard_map/all_to_all | solution.py:123

commit v3 on v2

--- a/solution.py
+++ b/solution.py
@@ -8,24 +8,19 @@
 
 
 def local_attention(query, new_key, new_value, key_cache, value_cache, lengths):
-    row_count = query.shape[0]
     local_width = query.shape[1]
     head_count = local_width // HD
     cache_len = key_cache.shape[1]
     score_scale = HD ** (-0.5)
-    queries = query.reshape(row_count, head_count, HD)
-    cached_keys = key_cache.reshape(row_count, cache_len, head_count, HD)
-    cached_values = value_cache.reshape(row_count, cache_len, head_count, HD)
+    lane_head = jnp.arange(local_width, dtype=jnp.int32) // HD
+    head_mask = lane_head[None, :] == jnp.arange(head_count, dtype=jnp.int32)[:, None]
+    masked_query = jnp.where(head_mask[None], query[:, None, :], jnp.zeros((), query.dtype))
     scores = (
-        jnp.einsum("rhd,rjhd->rhj", queries, cached_keys, preferred_element_type=jnp.float32)
+        jnp.einsum("rhf,rjf->rhj", masked_query, key_cache, preferred_element_type=jnp.float32)
         * score_scale
     )
     own_score = (
-        jnp.sum(
-            queries.astype(jnp.float32)
-            * new_key.reshape(row_count, head_count, HD).astype(jnp.float32),
-            axis=-1,
-        )
+        jnp.einsum("rhf,rf->rh", masked_query, new_key, preferred_element_type=jnp.float32)
         * score_scale
     )
     positions = jnp.arange(cache_len, dtype=jnp.int32)
@@ -37,13 +32,13 @@
     denominator = jnp.sum(cached_exp, axis=-1) + own_exp
     cached_prob = (cached_exp / denominator[..., None]).astype(jnp.bfloat16)
     own_prob = (own_exp / denominator).astype(jnp.bfloat16)
-    mixed_values = jnp.einsum(
-        "rhj,rjhd->rhd", cached_prob, cached_values, preferred_element_type=jnp.float32
+    mixed_heads = jnp.einsum(
+        "rhj,rjf->rhf", cached_prob, value_cache, preferred_element_type=jnp.float32
     )
-    mixed_values = mixed_values + own_prob.astype(jnp.float32)[..., None] * new_value.reshape(
-        row_count, head_count, HD
-    ).astype(jnp.float32)
-    return mixed_values.reshape(row_count, local_width).astype(jnp.bfloat16)
+    mixed_values = jnp.sum(jnp.where(head_mask[None], mixed_heads, 0.0), axis=1)
+    own_lanes = jnp.repeat(own_prob.astype(jnp.float32), HD, axis=1)
+    mixed_values = mixed_values + own_lanes * new_value.astype(jnp.float32)
+    return mixed_values.astype(jnp.bfloat16)
 
 
 def slot_tables(block_ids, block_weights, capacity):

time: 132 us -> 129 us (0.977)
  local copies, waits for them, and re-layouts: 15.5 us -> 12.1 us
  matrix products: 7.33 us -> 8.85 us
    convert_element_type x3 -> x0, local copies, waits for them, and re-layouts: 1.69 us -> none  [the longest x1 0.8 us: local_attention(): new_key.reshape(row_count, head_count, HD).astype(jnp.float32)]
    reshape x2 -> x1, local copies, waits for them, and re-layouts: 1.71 us -> 0.1 us  [local_attention(): own_lanes = jnp.repeat(own_prob.astype(jnp.float32), HD, axis=1)]
    dot_general x2 -> x3, matrix products: 2.77 us -> 3.62 us  [the longest x1 1.42 us: local_attention(): jnp.einsum('rhj,rjf->rhf', cached_prob, value_cache, preferred_element_ty...]
where the time goes in v3:
time: 129 us
  waiting for transfers between devices  43.6 us (34%)
  starting transfers between devices  32.2 us (25%)
  blocking collectives  29.6 us (23%)
  local copies, waits for them, and re-layouts  12.1 us (9%)
  matrix products  8.85 us (7%)
  other arithmetic  2.35 us (2%)
    all_to_all x1, waiting for transfers between devices, shards(): lax.all_to_all(partial_out, 'req', split_axis=0, concat_axis=0, tiled=True)  24.6 us
    all_to_all x1, starting transfers between devices, shards(): lax.all_to_all(outgoing, 'req', split_axis=0, concat_axis=0, tiled=True)  22.7 us
    all_to_all x1, waiting for transfers between devices, shards(): lax.all_to_all(outgoing, 'req', split_axis=0, concat_axis=0, tiled=True)  19 us
    all_to_all x1, blocking collectives, shards(): both = lax.all_to_all(both, 'tp', split_axis=0, concat_axis=0, tiled=True)  10.8 us
    all_gather x1, blocking collectives, shards(): proj_all = lax.all_gather(proj_part, 'tp', axis=0, tiled=False)  9.52 us
    all_to_all x1, starting transfers between devices, shards(): lax.all_to_all(partial_out, 'req', split_axis=0, concat_axis=0, tiled=True)  9.44 us
    all_gather x1, blocking collectives, shards(): activ = lax.all_gather(activ_chunk, 'tp', axis=1, tiled=True)  9.24 us
    another operation x2, local copies, waits for them, and re-layouts  3.08 us
  transfers between devices with their start and end apart: 2, of which 2 were waited for; matrix products, arithmetic and copies ran while one was open for 5% of the time, Pallas kernels for 0%

profile of v3, /device:TPU:33, one launch (start us, length us, event | category | flops | bytes accessed | tf_op | source)
XLA Modules:
  0.0 128.8 jit_solution(9250581662820925970)
XLA Ops:
  0.0 0.0 copy-start
  0.0 0.9 constant_dynamic-slice_fusion.1
  0.9 0.1 copy.54
  1.0 0.1 iota_compare_fusion.2
  1.1 0.7 iota_compare_fusion.4
  1.8 0.8 fusion.8
  2.7 1.4 %fusion.39 = (f32[4,9]{1,0:T(4,128)S(1)}, f32[4,9,128]{2,1,0:T(8,128)S(1)}) fusion(bf16[4,128,576]{1,2,0:T(8,128)(2,1)} %param.17, pred[9,576]{1,0:T(8,128)(4,1)S(1)} %iota_compare_fusion, bf16[4,576]{1,0:T(4,128)(2,1)} %param.14, pred[4,128]{1,0:T(4,128)(4,1)S(1)} %iota_compare_fusion.4), kind=kOutput, calls=%fused_computation.75 | convolution fusion | flops 5342940 | bytes 618704 | tf_op jit(solution)/shard_map/rhf,rjf->rhj/dot_general | solution.py:19
  4.1 0.2 fusion.20
  4.3 0.1 broadcast_in_dim.83
  4.3 0.1 reshape.231
  4.4 1.4 %fusion.2 = f32[4,576]{1,0:T(4,128)S(1)} fusion(bf16[4,128,576]{1,2,0:T(8,128)(2,1)} %param.18, pred[9,576]{1,0:T(8,128)(4,1)S(1)} %iota_compare_fusion, f32[4,9,128]{2,1,0:T(8,128)S(1)} %get-tuple-element.12, f32[4,9]{1,0:T(4,128)S(1)} %get-tuple-element.10, f32[4,9]{1,0:T(4,128)S(1)} %multiply_maximum_fusion), kind=kOutput, calls=%fused_computation.7 | convolution fusion | flops 5361408 | bytes 622944 | tf_op jit(solution)/shard_map/rhj,rjf->rhf/dot_general | solution.py:35
  5.8 0.0 copy-done
  5.9 1.1 convolution_bitcast_fusion
  7.0 9.5 %all-gather.1 = f32[4,4,2304]{2,1,0:T(4,128)S(1)} all-gather(f32[1,4,2304]{2,1,0:T(4,128)S(1)} %convolution_bitcast_fusion), channel_id=2, replica_groups=mesh['req'=128,'tp'=4] {'tp'}, dimensions={0}, use_global_device_ids=true | all-gather | bytes 184320 | tf_op jit(solution)/shard_map/all_gather | solution.py:80
  16.6 0.0 copy-done.2
  16.6 0.1 multiply_reduce_fusion
  16.7 0.1 eq.91
  16.8 0.1 fusion.31
  16.9 0.2 select_reduce_fusion
  17.1 0.1 eq.95
  17.2 0.1 copy.55
  17.3 0.1 and_reduce_fusion
  17.4 0.2 convolution_convert_fusion.3
  17.6 0.9 broadcast_in_dim.86
  18.5 22.7 %all-to-all-start = ((bf16[128,2,576]{2,1,0:T(2,128)(2,1)}), bf16[128,2,576]{2,1,0:T(2,128)(2,1)}, u32[]{:S(2)}, u32[]{:S(2)}) async-start(bf16[128,2,576]{2,1,0:T(2,128)(2,1)} %bitcast.5), calls=%async_computation | async-start | bytes 655360 | tf_op jit(solution)/shard_map/all_to_all | solution.py:97
  41.3 1.0 copy.57
  42.3 1.1 reshape.234
  43.4 2.0 %copy.59 = bf16[360,576]{1,0:T(8,128)(2,1)} copy(bf16[360,576]{0,1:T(8,128)(2,1)} %bitcast.58) | data formatting | bytes 829440 | tf_op jit(solution)/shard_map/dot_general | solution.py:100
  45.4 1.9 %reshape.235 = bf16[4,90,576]{2,1,0:T(8,128)(2,1)} reshape(bf16[360,576]{1,0:T(8,128)(2,1)} %copy.59) | data formatting | bytes 829440 | tf_op jit(solution)/shard_map/reshape.101
  47.4 19.0 %all-to-all-done = bf16[128,2,576]{2,1,0:T(2,128)(2,1)} async-done(((bf16[128,2,576]{2,1,0:T(2,128)(2,1)}), bf16[128,2,576]{2,1,0:T(2,128)(2,1)}, u32[]{:S(2)}, u32[]{:S(2)}) %all-to-all-start) | async-done | bytes 294944 | tf_op jit(solution)/shard_map/all_to_all | solution.py:97
  66.4 1.2 reshape.233
  67.6 0.3 fusion
  68.0 1.4 %fusion.1 = bf16[256,4,1,90]{0,3,1,2:T(8,128)(2,1)S(1)} fusion(bf16[4,90,576]{2,1,0:T(8,128)(2,1)} %reshape.235, bf16[256,576]{1,0:T(8,128)(2,1)S(1)} %reshape.233), kind=kOutput, calls=%fused_computation.5 | convolution fusion | flops 106260480 | bytes 893952 | tf_op jit(solution)/shard_map/dot_general | solution.py:100
  69.4 0.4 copy.61
  69.8 10.8 %all_to_all.15 = bf16[4,256,2,90]{1,2,3,0:T(2,128)(2,1)S(1)} all-to-all(bf16[4,256,2,90]{1,2,3,0:T(2,128)(2,1)S(1)} %copy.61), channel_id=1, replica_groups=mesh['req'=128,'tp'=4] {'tp'}, dimensions={0} | all-to-all | bytes 737280 | tf_op jit(solution)/shard_map/all_to_all | solution.py:109
  80.6 0.3 convert_reduce_fusion
  80.9 0.1 fusion.38
  81.1 9.2 %all-gather.2 = bf16[4,90,256]{2,1,0:T(8,128)(2,1)S(1)} all-gather(bf16[1,90,256]{2,1,0:T(8,128)(2,1)S(1)} %fusion.14), channel_id=1, replica_groups=mesh['req'=128,'tp'=4] {'tp'}, dimensions={0}, use_global_device_ids=true | all-gather | bytes 230400 | tf_op jit(solution)/shard_map/all_gather | solution.py:112
  90.4 0.1 reshape.242
  90.4 1.3 %convolution_convert_fusion = bf16[256,576]{0,1:T(8,128)(2,1)S(1)} fusion(bf16[360,256]{1,0:T(8,128)(2,1)S(1)} %reshape.242, bf16[360,576]{0,1:T(8,128)(2,1)} %param.27), kind=kOutput, calls=%fused_computation.1 | convolution fusion | flops 106315776 | bytes 893952 | tf_op jit(solution)/shard_map/dot_general | solution.py:114
  91.7 0.2 copy.63
  91.9 0.9 reshape.236
  92.8 9.4 %all-to-all-start.2 = ((bf16[128,2,576]{2,1,0:T(2,128)(2,1)}), bf16[128,2,576]{2,1,0:T(2,128)(2,1)S(1)}, u32[]{:S(2)}, u32[]{:S(2)}) async-start(bf16[128,2,576]{2,1,0:T(2,128)(2,1)} %reshape.236), calls=%async_computation.2 | async-start | bytes 655360 | tf_op jit(solution)/shard_map/all_to_all | solution.py:118
  102.3 0.8 constant_dynamic-slice_fusion
  103.0 0.1 fusion.24
  103.1 24.6 %all-to-all-done.2 = bf16[128,2,576]{2,1,0:T(2,128)(2,1)S(1)} async-done(((bf16[128,2,576]{2,1,0:T(2,128)(2,1)}), bf16[128,2,576]{2,1,0:T(2,128)(2,1)S(1)}, u32[]{:S(2)}, u32[]{:S(2)}) %all-to-all-start.2) | async-done | bytes 294944 | tf_op jit(solution)/shard_map/all_to_all | solution.py:118
  127.7 0.3 convert_reduce_fusion.1
  127.9 0.8 fusion.5
  (16 shorter events, 0.2 us)
Async XLA Ops:
  0.0 5.9 %copy-start = (bf16[576,2304]{1,0:T(8,128)(2,1)S(1)}, bf16[576,2304]{1,0:T(8,128)(2,1)}, u32[]{:S(2)}) copy-start(bf16[576,2304]{1,0:T(8,128)(2,1)} %param.21) | copy-start | bytes 7962628
  0.0 16.6 %copy-start.2 = (bf16[4,2304]{1,0:T(4,128)(2,1)S(1)}, bf16[4,2304]{1,0:T(4,128)(2,1)}, u32[]{:S(2)}) copy-start(bf16[4,2304]{1,0:T(4,128)(2,1)} %param.20) | copy-start | bytes 55300
  0.0 17.4 %copy-start.3 = (f32[576]{0:T(1024)S(1)}, f32[576]{0:T(1024)}, u32[]{:S(2)}) copy-start(f32[576]{0:T(1024)} %param.22) | copy-start | bytes 6916
  4.0 37.2 %copy-start.1 = (bf16[576,360]{1,0:T(8,128)(2,1)S(1)}, bf16[576,360]{1,0:T(8,128)(2,1)}, u32[]{:S(2)}) copy-start(bf16[576,360]{1,0:T(8,128)(2,1)} %param.25) | copy-start | bytes 1244164
  18.5 47.9 %all-to-all-start = ((bf16[128,2,576]{2,1,0:T(2,128)(2,1)}), bf16[128,2,576]{2,1,0:T(2,128)(2,1)}, u32[]{:S(2)}, u32[]{:S(2)}) async-start(bf16[128,2,576]{2,1,0:T(2,128)(2,1)} %bitcast.5), calls=%async_computation | async-start | bytes 655360 | tf_op jit(solution)/shard_map/all_to_all | solution.py:97
  92.8 34.9 %all-to-all-start.2 = ((bf16[128,2,576]{2,1,0:T(2,128)(2,1)}), bf16[128,2,576]{2,1,0:T(2,128)(2,1)S(1)}, u32[]{:S(2)}, u32[]{:S(2)}) async-start(bf16[128,2,576]{2,1,0:T(2,128)(2,1)} %reshape.236), calls=%async_computation.2 | async-start | bytes 655360 | tf_op jit(solution)/shard_map/all_to_all | solution.py:118

commit v4 on v3

--- a/solution.py
+++ b/solution.py
@@ -2,43 +2,76 @@
 import jax.numpy as jnp
 from jax import lax
 from jax.sharding import PartitionSpec as P
+from jax.experimental import pallas as pl
+from jax.experimental.pallas import tpu as pltpu
 
 HD = 64
 EXPERTS = 8
 
 
+def attention_kernel(len_ref, q_ref, nk_ref, nv_ref, k_ref, v_ref, o_ref):
+    row_count, local_width = q_ref.shape
+    head_count = local_width // HD
+    cache_len = k_ref.shape[2]
+    score_scale = HD ** (-0.5)
+    lane_head = lax.broadcasted_iota(jnp.int32, (head_count, local_width), 1) // HD
+    head_mask = lane_head == lax.broadcasted_iota(jnp.int32, (head_count, local_width), 0)
+    positions = lax.broadcasted_iota(jnp.int32, (head_count, cache_len), 1)
+    queries = q_ref[...].astype(jnp.float32)
+    new_keys = nk_ref[...].astype(jnp.float32)
+    new_values = nv_ref[...].astype(jnp.float32)
+    for r in range(row_count):
+        query_row = queries[r : r + 1, :]
+        masked_query = jnp.where(head_mask, query_row, 0.0)
+        scores = (
+            lax.dot_general(
+                masked_query.astype(jnp.bfloat16),
+                k_ref[r],
+                (((1,), (0,)), ((), ())),
+                preferred_element_type=jnp.float32,
+            )
+            * score_scale
+        )
+        own_score = (
+            jnp.sum(masked_query * new_keys[r : r + 1, :], axis=1, keepdims=True) * score_scale
+        )
+        scores = jnp.where(positions < len_ref[r], scores, -jnp.inf)
+        highest = jnp.maximum(jnp.max(scores, axis=1, keepdims=True), own_score)
+        cached_exp = jnp.exp(scores - highest)
+        own_exp = jnp.exp(own_score - highest)
+        denominator = jnp.sum(cached_exp, axis=1, keepdims=True) + own_exp
+        cached_prob = (cached_exp / denominator).astype(jnp.bfloat16)
+        own_prob = (own_exp / denominator).astype(jnp.bfloat16).astype(jnp.float32)
+        mixed_heads = lax.dot_general(
+            cached_prob, v_ref[r], (((1,), (1,)), ((), ())), preferred_element_type=jnp.float32
+        )
+        mixed = jnp.sum(jnp.where(head_mask, mixed_heads, 0.0), axis=0, keepdims=True)
+        own_lanes = jnp.sum(jnp.where(head_mask, own_prob, 0.0), axis=0, keepdims=True)
+        o_ref[r : r + 1, :] = (mixed + own_lanes * new_values[r : r + 1, :]).astype(o_ref.dtype)
+
+
 def local_attention(query, new_key, new_value, key_cache, value_cache, lengths):
-    local_width = query.shape[1]
-    head_count = local_width // HD
+    row_count, local_width = query.shape
     cache_len = key_cache.shape[1]
-    score_scale = HD ** (-0.5)
-    lane_head = jnp.arange(local_width, dtype=jnp.int32) // HD
-    head_mask = lane_head[None, :] == jnp.arange(head_count, dtype=jnp.int32)[:, None]
-    masked_query = jnp.where(head_mask[None], query[:, None, :], jnp.zeros((), query.dtype))
-    scores = (
-        jnp.einsum("rhf,rjf->rhj", masked_query, key_cache, preferred_element_type=jnp.float32)
-        * score_scale
+    vmem = pl.BlockSpec(memory_space=pltpu.VMEM)
+    return pl.pallas_call(
+        attention_kernel,
+        out_shape=jax.ShapeDtypeStruct((row_count, local_width), jnp.bfloat16),
+        in_specs=[pl.BlockSpec(memory_space=pltpu.SMEM)] + [vmem] * 5,
+        out_specs=vmem,
+        cost_estimate=pl.CostEstimate(
+            flops=4 * row_count * (local_width // HD) * cache_len * local_width,
+            transcendentals=row_count * (local_width // HD) * (cache_len + 1),
+            bytes_accessed=2 * key_cache.size * 2 + 4 * query.size * 2,
+        ),
+    )(
+        lengths,
+        query,
+        new_key,
+        new_value,
+        jnp.swapaxes(key_cache, 1, 2),
+        jnp.swapaxes(value_cache, 1, 2),
     )
-    own_score = (
-        jnp.einsum("rhf,rf->rh", masked_query, new_key, preferred_element_type=jnp.float32)
-        * score_scale
-    )
-    positions = jnp.arange(cache_len, dtype=jnp.int32)
-    is_valid = positions[None, None, :] < lengths[:, None, None]
-    scores = jnp.where(is_valid, scores, -jnp.inf)
-    highest = jnp.maximum(jnp.max(scores, axis=-1), own_score)
-    cached_exp = jnp.exp(scores - highest[..., None])
-    own_exp = jnp.exp(own_score - highest)
-    denominator = jnp.sum(cached_exp, axis=-1) + own_exp
-    cached_prob = (cached_exp / denominator[..., None]).astype(jnp.bfloat16)
-    own_prob = (own_exp / denominator).astype(jnp.bfloat16)
-    mixed_heads = jnp.einsum(
-        "rhj,rjf->rhf", cached_prob, value_cache, preferred_element_type=jnp.float32
-    )
-    mixed_values = jnp.sum(jnp.where(head_mask[None], mixed_heads, 0.0), axis=1)
-    own_lanes = jnp.repeat(own_prob.astype(jnp.float32), HD, axis=1)
-    mixed_values = mixed_values + own_lanes * new_value.astype(jnp.float32)
-    return mixed_values.astype(jnp.bfloat16)
 
 
 def slot_tables(block_ids, block_weights, capacity):

time: 129 us -> 128 us (level)
  matrix products: 8.85 us -> 5.24 us
  Pallas kernels: 0 us -> 3.38 us
    dot_general x3 -> x0, matrix products: 3.62 us -> none  [the longest x1 1.42 us: local_attention(): jnp.einsum('rhj,rjf->rhf', cached_prob, value_cache, preferred_element_ty...]
    pallas_call x0 -> x1, Pallas kernels: none -> 3.38 us  [local_attention(): pl.pallas_call(attention_kernel, out_shape=jax.ShapeDtypeStruct((row_coun...]
where the time goes in v4:
time: 128 us; the launch traced here: 127 us
  waiting for transfers between devices  43.6 us (34%)
  starting transfers between devices  32.2 us (25%)
  blocking collectives  29.6 us (23%)
  local copies, waits for them, and re-layouts  11.9 us (9%)
  matrix products  5.24 us (4%)
  Pallas kernels  3.38 us (3%)
  other arithmetic  1.41 us (1%)
    all_to_all x1, waiting for transfers between devices, shards(): lax.all_to_all(partial_out, 'req', split_axis=0, concat_axis=0, tiled=True)  24.6 us
    all_to_all x1, starting transfers between devices, shards(): lax.all_to_all(outgoing, 'req', split_axis=0, concat_axis=0, tiled=True)  22.7 us
    all_to_all x1, waiting for transfers between devices, shards(): lax.all_to_all(outgoing, 'req', split_axis=0, concat_axis=0, tiled=True)  19 us
    all_to_all x1, blocking collectives, shards(): both = lax.all_to_all(both, 'tp', split_axis=0, concat_axis=0, tiled=True)  10.8 us
    all_gather x1, blocking collectives, shards(): proj_all = lax.all_gather(proj_part, 'tp', axis=0, tiled=False)  9.52 us
    all_to_all x1, starting transfers between devices, shards(): lax.all_to_all(partial_out, 'req', split_axis=0, concat_axis=0, tiled=True)  9.44 us
    all_gather x1, blocking collectives, shards(): activ = lax.all_gather(activ_chunk, 'tp', axis=1, tiled=True)  9.24 us
    pallas_call x1, Pallas kernels, local_attention(): pl.pallas_call(attention_kernel, out_shape=jax.ShapeDtypeStruct((row_coun...  3.38 us
  transfers between devices with their start and end apart: 2, of which 2 were waited for; matrix products, arithmetic and copies ran while one was open for 5% of the time, Pallas kernels for 0%

profile of v4, /device:TPU:33, one launch (start us, length us, event | category | flops | bytes accessed | tf_op | source)
XLA Modules:
  0.0 127.4 jit_solution(9524461667451847080)
XLA Ops:
  0.0 0.0 copy-start
  0.0 0.0 copy-start.2
  0.0 0.0 copy-start.3
  0.0 0.9 constant_dynamic-slice_fusion.1
  0.9 0.1 copy.54
  1.0 0.1 iota_compare_fusion.1
  1.1 0.1 eq.65
  1.2 0.1 fusion.14
  1.3 0.2 select_reduce_fusion
  1.5 0.1 eq.69
  1.5 0.1 copy.55
  1.7 0.0 copy-start.1
  1.7 3.4 %shard_map.136 = bf16[4,576]{1,0:T(4,128)(2,1)} custom-call(s32[4]{0:T(128)} %len_ref.1, bf16[4,576]{1,0:T(4,128)(2,1)} %q_ref.1, bf16[4,576]{1,0:T(4,128)(2,1)} %nk_ref.1, bf16[4,576]{1,0:T(4,128)(2,1)} %nv_ref.1, bf16[4,576,128]{2,1,0:T(8,128)(2,1)} %bitcast.55, bf16[4,576,128]{2,1,0:T(8,128)(2,1)} %bitcast.56), custom_call_target="tpu_custom_call" | custom-call | flops 10616832 | bytes 1198080 | tf_op jit(solution)/shard_map/pallas_call | solution.py:57
  5.0 0.0 copy-done
  5.0 1.1 convolution_bitcast_fusion
  6.2 9.5 %all-gather.1 = f32[4,4,2304]{2,1,0:T(4,128)S(1)} all-gather(f32[1,4,2304]{2,1,0:T(4,128)S(1)} %convolution_bitcast_fusion), channel_id=2, replica_groups=mesh['req'=128,'tp'=4] {'tp'}, dimensions={0}, use_global_device_ids=true | all-gather | bytes 184320 | tf_op jit(solution)/shard_map/all_gather | solution.py:113
  15.7 0.0 copy-done.2
  15.7 0.1 multiply_reduce_fusion
  15.9 0.1 and_reduce_fusion
  16.0 0.0 copy-done.3
  16.0 0.2 convolution_convert_fusion.3
  16.2 0.9 broadcast_in_dim.23
  17.1 22.7 %all-to-all-start = ((bf16[128,2,576]{2,1,0:T(2,128)(2,1)}), bf16[128,2,576]{2,1,0:T(2,128)(2,1)}, u32[]{:S(2)}, u32[]{:S(2)}) async-start(bf16[128,2,576]{2,1,0:T(2,128)(2,1)} %bitcast.4), calls=%async_computation | async-start | bytes 655360 | tf_op jit(solution)/shard_map/all_to_all | solution.py:130
  39.9 0.0 copy-done.1
  39.9 1.0 copy.57
  40.9 1.1 reshape.173
  42.0 2.0 %copy.59 = bf16[360,576]{1,0:T(8,128)(2,1)} copy(bf16[360,576]{0,1:T(8,128)(2,1)} %bitcast.58) | data formatting | bytes 829440 | tf_op jit(solution)/shard_map/dot_general | solution.py:133
  44.0 1.9 %reshape.174 = bf16[4,90,576]{2,1,0:T(8,128)(2,1)} reshape(bf16[360,576]{1,0:T(8,128)(2,1)} %copy.59) | data formatting | bytes 829440 | tf_op jit(solution)/shard_map/reshape.74
  46.0 19.0 %all-to-all-done = bf16[128,2,576]{2,1,0:T(2,128)(2,1)} async-done(((bf16[128,2,576]{2,1,0:T(2,128)(2,1)}), bf16[128,2,576]{2,1,0:T(2,128)(2,1)}, u32[]{:S(2)}, u32[]{:S(2)}) %all-to-all-start) | async-done | bytes 294944 | tf_op jit(solution)/shard_map/all_to_all | solution.py:130
  65.0 1.2 reshape.172
  66.2 0.3 fusion
  66.6 1.4 %fusion.1 = bf16[256,4,1,90]{0,3,1,2:T(8,128)(2,1)S(1)} fusion(bf16[4,90,576]{2,1,0:T(8,128)(2,1)} %reshape.174, bf16[256,576]{1,0:T(8,128)(2,1)S(1)} %reshape.172), kind=kOutput, calls=%fused_computation.5 | convolution fusion | flops 106260480 | bytes 893952 | tf_op jit(solution)/shard_map/dot_general | solution.py:133
  68.0 0.4 copy.61
  68.4 10.8 %all_to_all.15 = bf16[4,256,2,90]{1,2,3,0:T(2,128)(2,1)S(1)} all-to-all(bf16[4,256,2,90]{1,2,3,0:T(2,128)(2,1)S(1)} %copy.61), channel_id=1, replica_groups=mesh['req'=128,'tp'=4] {'tp'}, dimensions={0} | all-to-all | bytes 737280 | tf_op jit(solution)/shard_map/all_to_all | solution.py:142
  79.2 0.3 convert_reduce_fusion
  79.5 0.1 fusion.16
  79.7 9.2 %all-gather.2 = bf16[4,90,256]{2,1,0:T(8,128)(2,1)S(1)} all-gather(bf16[1,90,256]{2,1,0:T(8,128)(2,1)S(1)} %fusion.7), channel_id=1, replica_groups=mesh['req'=128,'tp'=4] {'tp'}, dimensions={0}, use_global_device_ids=true | all-gather | bytes 230400 | tf_op jit(solution)/shard_map/all_gather | solution.py:145
  89.0 0.1 reshape.181
  89.0 1.3 %convolution_convert_fusion = bf16[256,576]{0,1:T(8,128)(2,1)S(1)} fusion(bf16[360,256]{1,0:T(8,128)(2,1)S(1)} %reshape.181, bf16[360,576]{0,1:T(8,128)(2,1)} %param.27), kind=kOutput, calls=%fused_computation.1 | convolution fusion | flops 106315776 | bytes 893952 | tf_op jit(solution)/shard_map/dot_general | solution.py:147
  90.4 0.2 copy.63
  90.6 0.9 reshape.175
  91.4 9.4 %all-to-all-start.2 = ((bf16[128,2,576]{2,1,0:T(2,128)(2,1)}), bf16[128,2,576]{2,1,0:T(2,128)(2,1)S(1)}, u32[]{:S(2)}, u32[]{:S(2)}) async-start(bf16[128,2,576]{2,1,0:T(2,128)(2,1)} %reshape.175), calls=%async_computation.2 | async-start | bytes 655360 | tf_op jit(solution)/shard_map/all_to_all | solution.py:151
  100.9 0.8 constant_dynamic-slice_fusion
  101.6 0.1 fusion.9
  101.7 24.6 %all-to-all-done.2 = bf16[128,2,576]{2,1,0:T(2,128)(2,1)S(1)} async-done(((bf16[128,2,576]{2,1,0:T(2,128)(2,1)}), bf16[128,2,576]{2,1,0:T(2,128)(2,1)S(1)}, u32[]{:S(2)}, u32[]{:S(2)}) %all-to-all-start.2) | async-done | bytes 294944 | tf_op jit(solution)/shard_map/all_to_all | solution.py:151
  126.3 0.3 convert_reduce_fusion.1
  126.5 0.8 fusion.3
  (7 shorter events, 0.2 us)
Async XLA Ops:
  0.0 5.0 %copy-start = (bf16[576,2304]{1,0:T(8,128)(2,1)S(1)}, bf16[576,2304]{1,0:T(8,128)(2,1)}, u32[]{:S(2)}) copy-start(bf16[576,2304]{1,0:T(8,128)(2,1)} %param.21) | copy-start | bytes 7962628
  0.0 15.7 %copy-start.2 = (bf16[4,2304]{1,0:T(4,128)(2,1)S(1)}, bf16[4,2304]{1,0:T(4,128)(2,1)}, u32[]{:S(2)}) copy-start(bf16[4,2304]{1,0:T(4,128)(2,1)} %param.20) | copy-start | bytes 55300
  0.0 16.0 %copy-start.3 = (f32[576]{0:T(1024)S(1)}, f32[576]{0:T(1024)}, u32[]{:S(2)}) copy-start(f32[576]{0:T(1024)} %param.22) | copy-start | bytes 6916
  1.7 38.2 %copy-start.1 = (bf16[576,360]{1,0:T(8,128)(2,1)S(1)}, bf16[576,360]{1,0:T(8,128)(2,1)}, u32[]{:S(2)}) copy-start(bf16[576,360]{1,0:T(8,128)(2,1)} %param.25) | copy-start | bytes 1244164
  17.1 47.9 %all-to-all-start = ((bf16[128,2,576]{2,1,0:T(2,128)(2,1)}), bf16[128,2,576]{2,1,0:T(2,128)(2,1)}, u32[]{:S(2)}, u32[]{:S(2)}) async-start(bf16[128,2,576]{2,1,0:T(2,128)(2,1)} %bitcast.4), calls=%async_computation | async-start | bytes 655360 | tf_op jit(solution)/shard_map/all_to_all | solution.py:130
  91.4 34.8 %all-to-all-start.2 = ((bf16[128,2,576]{2,1,0:T(2,128)(2,1)}), bf16[128,2,576]{2,1,0:T(2,128)(2,1)S(1)}, u32[]{:S(2)}, u32[]{:S(2)}) async-start(bf16[128,2,576]{2,1,0:T(2,128)(2,1)} %reshape.175), calls=%async_computation.2 | async-start | bytes 655360 | tf_op jit(solution)/shard_map/all_to_all | solution.py:151

commit v5 on v4

--- a/solution.py
+++ b/solution.py
@@ -129,18 +129,21 @@
     outgoing = jnp.repeat(expert_rows, group_size, axis=0)
     arrived = lax.all_to_all(outgoing, "req", split_axis=0, concat_axis=0, tiled=True)
     token_rows = arrived.reshape(req_count * capacity, share)
-    gate_part = jnp.dot(token_rows, gate_weight, preferred_element_type=jnp.float32)
-    up_part = jnp.dot(token_rows, up_weight, preferred_element_type=jnp.float32)
     tp_count = lax.axis_size("tp")
-    slot_count = token_rows.shape[0]
-    chunk = gate_part.shape[1] // tp_count
-    both = jnp.stack(
-        [gate_part.reshape(slot_count, tp_count, chunk), up_part.reshape(slot_count, tp_count, chunk)],
+    chunk = gate_weight.shape[1] // tp_count
+    paired_weight = jnp.concatenate(
+        [
+            gate_weight.reshape(share, tp_count, chunk),
+            up_weight.reshape(share, tp_count, chunk),
+        ],
         axis=2,
     )
-    both = jnp.moveaxis(both, 1, 0).astype(jnp.bfloat16)
+    both = jnp.einsum(
+        "sf,ftk->tsk", token_rows, paired_weight, preferred_element_type=jnp.float32
+    ).astype(jnp.bfloat16)
     both = lax.all_to_all(both, "tp", split_axis=0, concat_axis=0, tiled=True)
     summed = jnp.sum(both.astype(jnp.float32), axis=0)
+    summed = jnp.stack([summed[:, :chunk], summed[:, chunk:]], axis=1)
     activ_chunk = (jax.nn.silu(summed[:, 0]) * summed[:, 1]).astype(jnp.bfloat16)
     activ = lax.all_gather(activ_chunk, "tp", axis=1, tiled=True)
     partial_out = (

time: 128 us -> 126 us (0.984)
  local copies, waits for them, and re-layouts: 11.9 us -> 8.64 us
  waiting for transfers between devices: 43.6 us -> 45.6 us
    another operation x2 -> x0, local copies, waits for them, and re-layouts: 3.08 us -> none
    dot_general x2 -> x0, local copies, waits for them, and re-layouts: 3 us -> none  [the longest x1 2 us: shards(): up_part = jnp.dot(token_rows, up_weight, preferred_element_type=jnp.float32)]
    unnamed x9, local copies, waits for them, and re-layouts: 0.07 us -> 2.57 us
    all_to_all x1, waiting for transfers between devices: 19 us -> 21.1 us  [shards(): lax.all_to_all(outgoing, 'req', split_axis=0, concat_axis=0, tiled=True)]
    reshape x0 -> x2, local copies, waits for them, and re-layouts: none -> 1.83 us  [the longest x1 0.92 us: shards(): gate_weight.reshape(share, tp_count, chunk)]
  transfers between devices with their start and end apart: 2 -> 2, of which waited for: 2 -> 2; matrix products, arithmetic and copies ran while one was open for 5% -> 4% of each run, Pallas kernels for 0% -> 0%
where the time goes in v5:
time: 126 us; the launch traced here: 125 us
  waiting for transfers between devices  45.6 us (36%)
  starting transfers between devices  31.8 us (25%)
  blocking collectives  29.6 us (23%)
  local copies, waits for them, and re-layouts  8.64 us (7%)
  matrix products  5.2 us (4%)
  Pallas kernels  3.32 us (3%)
    all_to_all x1, waiting for transfers between devices, shards(): lax.all_to_all(partial_out, 'req', split_axis=0, concat_axis=0, tiled=True)  24.6 us
    all_to_all x1, starting transfers between devices, shards(): lax.all_to_all(outgoing, 'req', split_axis=0, concat_axis=0, tiled=True)  22.3 us
    all_to_all x1, waiting for transfers between devices, shards(): lax.all_to_all(outgoing, 'req', split_axis=0, concat_axis=0, tiled=True)  21.1 us
    all_to_all x1, blocking collectives, shards(): both = lax.all_to_all(both, 'tp', split_axis=0, concat_axis=0, tiled=True)  10.9 us
    all_gather x1, blocking collectives, shards(): proj_all = lax.all_gather(proj_part, 'tp', axis=0, tiled=False)  9.52 us
    all_to_all x1, starting transfers between devices, shards(): lax.all_to_all(partial_out, 'req', split_axis=0, concat_axis=0, tiled=True)  9.46 us
    all_gather x1, blocking collectives, shards(): activ = lax.all_gather(activ_chunk, 'tp', axis=1, tiled=True)  9.24 us
    pallas_call x1, Pallas kernels, local_attention(): pl.pallas_call(attention_kernel, out_shape=jax.ShapeDtypeStruct((row_coun...  3.32 us
  transfers between devices with their start and end apart: 2, of which 2 were waited for; matrix products, arithmetic and copies ran while one was open for 4% of the time, Pallas kernels for 0%

profile of v5, /device:TPU:33, one launch (start us, length us, event | category | flops | bytes accessed | tf_op | source)
XLA Modules:
  0.0 125.4 jit_solution(12710604986749320945)
XLA Ops:
  0.0 0.0 copy-start
  0.0 0.0 copy-start.1
  0.0 0.0 copy-start.2
  0.0 0.9 constant_dynamic-slice_fusion.1
  0.9 0.1 copy.38
  1.0 0.1 iota_compare_fusion.1
  1.1 0.1 eq.65
  1.2 0.1 fusion.15
  1.3 0.2 select_reduce_fusion
  1.5 0.1 eq.69
  1.5 0.1 copy.39
  1.7 3.3 %shard_map.136 = bf16[4,576]{1,0:T(4,128)(2,1)} custom-call(s32[4]{0:T(128)} %len_ref.1, bf16[4,576]{1,0:T(4,128)(2,1)} %q_ref.1, bf16[4,576]{1,0:T(4,128)(2,1)} %nk_ref.1, bf16[4,576]{1,0:T(4,128)(2,1)} %nv_ref.1, bf16[4,576,128]{2,1,0:T(8,128)(2,1)} %bitcast.36, bf16[4,576,128]{2,1,0:T(8,128)(2,1)} %bitcast.37), custom_call_target="tpu_custom_call" | custom-call | flops 10616832 | bytes 1198080 | tf_op jit(solution)/shard_map/pallas_call | solution.py:57
  5.0 0.0 copy-done
  5.0 1.1 convolution_bitcast_fusion
  6.1 9.5 %all-gather.1 = f32[4,4,2304]{2,1,0:T(4,128)S(1)} all-gather(f32[1,4,2304]{2,1,0:T(4,128)S(1)} %convolution_bitcast_fusion), channel_id=2, replica_groups=mesh['req'=128,'tp'=4] {'tp'}, dimensions={0}, use_global_device_ids=true | all-gather | bytes 184320 | tf_op jit(solution)/shard_map/all_gather | solution.py:113
  15.7 0.0 copy-done.1
  15.7 0.1 multiply_reduce_fusion
  15.8 0.1 and_reduce_fusion
  15.9 0.0 copy-done.2
  15.9 0.2 convolution_convert_fusion.2
  16.2 0.9 broadcast_in_dim.23
  17.1 22.3 %all-to-all-start = ((bf16[128,2,576]{2,1,0:T(2,128)(2,1)}), bf16[128,2,576]{2,1,0:T(2,128)(2,1)S(1)}, u32[]{:S(2)}, u32[]{:S(2)}) async-start(bf16[128,2,576]{2,1,0:T(2,128)(2,1)} %bitcast.4), calls=%async_computation | async-start | bytes 655360 | tf_op jit(solution)/shard_map/all_to_all | solution.py:130
  39.4 1.3 copy.41
  40.7 0.9 reshape.164
  41.6 1.2 copy.40
  42.8 0.9 reshape.163
  43.8 21.1 %all-to-all-done = bf16[128,2,576]{2,1,0:T(2,128)(2,1)S(1)} async-done(((bf16[128,2,576]{2,1,0:T(2,128)(2,1)}), bf16[128,2,576]{2,1,0:T(2,128)(2,1)S(1)}, u32[]{:S(2)}, u32[]{:S(2)}) %all-to-all-start) | async-done | bytes 294944 | tf_op jit(solution)/shard_map/all_to_all | solution.py:130
  64.8 0.2 reshape.166
  65.1 1.7 %fusion = bf16[4,256,180]{1,2,0:T(8,128)(2,1)S(1)} fusion(bf16[576,4,90]{0,2,1:T(8,128)(2,1)} %reshape.164, bf16[576,4,90]{0,2,1:T(8,128)(2,1)} %reshape.163, bf16[256,576]{1,0:T(8,128)(2,1)S(1)} %reshape.166), kind=kOutput, calls=%fused_computation.3 | convolution fusion | flops 214179840 | bytes 1492992 | tf_op jit(solution)/shard_map/sf,ftk->tsk/dot_general | solution.py:141
  66.8 10.9 %all_to_all.15 = bf16[4,256,180]{1,2,0:T(8,128)(2,1)S(1)} all-to-all(bf16[4,256,180]{1,2,0:T(8,128)(2,1)S(1)} %fusion), channel_id=1, replica_groups=mesh['req'=128,'tp'=4] {'tp'}, dimensions={0} | all-to-all | bytes 737280 | tf_op jit(solution)/shard_map/all_to_all | solution.py:144
  77.8 9.2 %all-gather.2 = bf16[4,90,256]{2,1,0:T(8,128)(2,1)S(1)} all-gather(bf16[1,90,256]{2,1,0:T(8,128)(2,1)S(1)} %fusion.8), channel_id=1, replica_groups=mesh['req'=128,'tp'=4] {'tp'}, dimensions={0}, use_global_device_ids=true | all-gather | bytes 230400 | tf_op jit(solution)/shard_map/all_gather | solution.py:148
  87.0 0.1 reshape.173
  87.1 1.3 %convolution_convert_fusion.1 = bf16[256,576]{0,1:T(8,128)(2,1)S(1)} fusion(bf16[360,256]{1,0:T(8,128)(2,1)S(1)} %reshape.173, bf16[360,576]{0,1:T(8,128)(2,1)} %param.27), kind=kOutput, calls=%fused_computation.2 | convolution fusion | flops 106315776 | bytes 893952 | tf_op jit(solution)/shard_map/dot_general | solution.py:150
  88.4 0.2 copy.44
  88.6 0.9 reshape.167
  89.4 9.5 %all-to-all-start.2 = ((bf16[128,2,576]{2,1,0:T(2,128)(2,1)}), bf16[128,2,576]{2,1,0:T(2,128)(2,1)S(1)}, u32[]{:S(2)}, u32[]{:S(2)}) async-start(bf16[128,2,576]{2,1,0:T(2,128)(2,1)} %reshape.167), calls=%async_computation.2 | async-start | bytes 655360 | tf_op jit(solution)/shard_map/all_to_all | solution.py:154
  98.9 0.8 constant_dynamic-slice_fusion
  99.7 0.1 fusion.10
  99.7 24.6 %all-to-all-done.2 = bf16[128,2,576]{2,1,0:T(2,128)(2,1)S(1)} async-done(((bf16[128,2,576]{2,1,0:T(2,128)(2,1)}), bf16[128,2,576]{2,1,0:T(2,128)(2,1)S(1)}, u32[]{:S(2)}, u32[]{:S(2)}) %all-to-all-start.2) | async-done | bytes 294944 | tf_op jit(solution)/shard_map/all_to_all | solution.py:154
  124.3 0.3 convert_reduce_fusion.1
  124.6 0.8 fusion.2
  (7 shorter events, 0.2 us)
Async XLA Ops:
  0.0 5.0 %copy-start = (bf16[576,2304]{1,0:T(8,128)(2,1)S(1)}, bf16[576,2304]{1,0:T(8,128)(2,1)}, u32[]{:S(2)}) copy-start(bf16[576,2304]{1,0:T(8,128)(2,1)} %param.21) | copy-start | bytes 7962628
  0.0 15.7 %copy-start.1 = (bf16[4,2304]{1,0:T(4,128)(2,1)S(1)}, bf16[4,2304]{1,0:T(4,128)(2,1)}, u32[]{:S(2)}) copy-start(bf16[4,2304]{1,0:T(4,128)(2,1)} %param.20) | copy-start | bytes 55300
  0.0 15.9 %copy-start.2 = (f32[576]{0:T(1024)S(1)}, f32[576]{0:T(1024)}, u32[]{:S(2)}) copy-start(f32[576]{0:T(1024)} %param.22) | copy-start | bytes 6916
  17.1 47.7 %all-to-all-start = ((bf16[128,2,576]{2,1,0:T(2,128)(2,1)}), bf16[128,2,576]{2,1,0:T(2,128)(2,1)S(1)}, u32[]{:S(2)}, u32[]{:S(2)}) async-start(bf16[128,2,576]{2,1,0:T(2,128)(2,1)} %bitcast.4), calls=%async_computation | async-start | bytes 655360 | tf_op jit(solution)/shard_map/all_to_all | solution.py:130
  89.4 34.9 %all-to-all-start.2 = ((bf16[128,2,576]{2,1,0:T(2,128)(2,1)}), bf16[128,2,576]{2,1,0:T(2,128)(2,1)S(1)}, u32[]{:S(2)}, u32[]{:S(2)}) async-start(bf16[128,2,576]{2,1,0:T(2,128)(2,1)} %reshape.167), calls=%async_computation.2 | async-start | bytes 655360 | tf_op jit(solution)/shard_map/all_to_all | solution.py:154

commit v6 on v5

--- a/solution.py
+++ b/solution.py
@@ -13,41 +13,49 @@
     row_count, local_width = q_ref.shape
     head_count = local_width // HD
     cache_len = k_ref.shape[2]
+    pair_count = row_count * head_count
     score_scale = HD ** (-0.5)
-    lane_head = lax.broadcasted_iota(jnp.int32, (head_count, local_width), 1) // HD
-    head_mask = lane_head == lax.broadcasted_iota(jnp.int32, (head_count, local_width), 0)
-    positions = lax.broadcasted_iota(jnp.int32, (head_count, cache_len), 1)
-    queries = q_ref[...].astype(jnp.float32)
-    new_keys = nk_ref[...].astype(jnp.float32)
+    pair_row = lax.broadcasted_iota(jnp.int32, (pair_count, row_count), 0) // head_count
+    pick_row = (pair_row == lax.broadcasted_iota(jnp.int32, (pair_count, row_count), 1)).astype(
+        jnp.bfloat16
+    )
+    lane_head = lax.broadcasted_iota(jnp.int32, (pair_count, local_width), 1) // HD
+    pair_head = lax.broadcasted_iota(jnp.int32, (pair_count, local_width), 0) % head_count
+    head_mask = lane_head == pair_head
+    query_rows = jnp.dot(pick_row, q_ref[...], preferred_element_type=jnp.float32)
+    new_key_rows = jnp.dot(pick_row, nk_ref[...], preferred_element_type=jnp.float32)
+    masked_query = jnp.where(head_mask, query_rows, 0.0)
+    all_keys = jnp.concatenate([k_ref[r] for r in range(row_count)], axis=1)
+    all_values = jnp.concatenate([v_ref[r] for r in range(row_count)], axis=1)
+    scores = (
+        jnp.dot(masked_query.astype(jnp.bfloat16), all_keys, preferred_element_type=jnp.float32)
+        * score_scale
+    )
+    own_score = jnp.sum(masked_query * new_key_rows, axis=1, keepdims=True) * score_scale
+    column = lax.broadcasted_iota(jnp.int32, (pair_count, row_count * cache_len), 1)
+    owner = lax.broadcasted_iota(jnp.int32, (pair_count, row_count * cache_len), 0) // head_count
+    row_length = jnp.zeros((pair_count, row_count * cache_len), jnp.int32)
+    for r in range(row_count):
+        row_length = jnp.where(owner == r, len_ref[r], row_length)
+    valid = (column // cache_len == owner) & (column % cache_len < row_length)
+    scores = jnp.where(valid, scores, -jnp.inf)
+    highest = jnp.maximum(jnp.max(scores, axis=1, keepdims=True), own_score)
+    cached_exp = jnp.exp(scores - highest)
+    own_exp = jnp.exp(own_score - highest)
+    denominator = jnp.sum(cached_exp, axis=1, keepdims=True) + own_exp
+    cached_prob = (cached_exp / denominator).astype(jnp.bfloat16)
+    own_prob = (own_exp / denominator).astype(jnp.bfloat16).astype(jnp.float32)
+    mixed_heads = lax.dot_general(
+        cached_prob, all_values, (((1,), (1,)), ((), ())), preferred_element_type=jnp.float32
+    )
+    mixed_heads = jnp.where(head_mask, mixed_heads, 0.0)
+    own_lanes = jnp.where(head_mask, own_prob, 0.0)
     new_values = nv_ref[...].astype(jnp.float32)
     for r in range(row_count):
-        query_row = queries[r : r + 1, :]
-        masked_query = jnp.where(head_mask, query_row, 0.0)
-        scores = (
-            lax.dot_general(
-                masked_query.astype(jnp.bfloat16),
-                k_ref[r],
-                (((1,), (0,)), ((), ())),
-                preferred_element_type=jnp.float32,
-            )
-            * score_scale
-        )
-        own_score = (
-            jnp.sum(masked_query * new_keys[r : r + 1, :], axis=1, keepdims=True) * score_scale
-        )
-        scores = jnp.where(positions < len_ref[r], scores, -jnp.inf)
-        highest = jnp.maximum(jnp.max(scores, axis=1, keepdims=True), own_score)
-        cached_exp = jnp.exp(scores - highest)
-        own_exp = jnp.exp(own_score - highest)
-        denominator = jnp.sum(cached_exp, axis=1, keepdims=True) + own_exp
-        cached_prob = (cached_exp / denominator).astype(jnp.bfloat16)
-        own_prob = (own_exp / denominator).astype(jnp.bfloat16).astype(jnp.float32)
-        mixed_heads = lax.dot_general(
-            cached_prob, v_ref[r], (((1,), (1,)), ((), ())), preferred_element_type=jnp.float32
-        )
-        mixed = jnp.sum(jnp.where(head_mask, mixed_heads, 0.0), axis=0, keepdims=True)
-        own_lanes = jnp.sum(jnp.where(head_mask, own_prob, 0.0), axis=0, keepdims=True)
-        o_ref[r : r + 1, :] = (mixed + own_lanes * new_values[r : r + 1, :]).astype(o_ref.dtype)
+        rows = slice(r * head_count, (r + 1) * head_count)
+        mixed = jnp.sum(mixed_heads[rows], axis=0, keepdims=True)
+        own = jnp.sum(own_lanes[rows], axis=0, keepdims=True)
+        o_ref[r : r + 1, :] = (mixed + own * new_values[r : r + 1, :]).astype(o_ref.dtype)
 
 
 def local_attention(query, new_key, new_value, key_cache, value_cache, lengths):

time: 126 us -> 125 us (level)
  no operation moved by 1% of the time
where the time goes in v6:
time: 125 us
  waiting for transfers between devices  45.6 us (36%)
  starting transfers between devices  31.8 us (25%)
  blocking collectives  29.6 us (24%)
  local copies, waits for them, and re-layouts  8.64 us (7%)
  matrix products  5.2 us (4%)
  Pallas kernels  2.68 us (2%)
    all_to_all x1, waiting for transfers between devices, shards(): lax.all_to_all(partial_out, 'req', split_axis=0, concat_axis=0, tiled=True)  24.6 us
    all_to_all x1, starting transfers between devices, shards(): lax.all_to_all(outgoing, 'req', split_axis=0, concat_axis=0, tiled=True)  22.3 us
    all_to_all x1, waiting for transfers between devices, shards(): lax.all_to_all(outgoing, 'req', split_axis=0, concat_axis=0, tiled=True)  21.1 us
    all_to_all x1, blocking collectives, shards(): both = lax.all_to_all(both, 'tp', split_axis=0, concat_axis=0, tiled=True)  10.9 us
    all_gather x1, blocking collectives, shards(): proj_all = lax.all_gather(proj_part, 'tp', axis=0, tiled=False)  9.52 us
    all_to_all x1, starting transfers between devices, shards(): lax.all_to_all(partial_out, 'req', split_axis=0, concat_axis=0, tiled=True)  9.46 us
    all_gather x1, blocking collectives, shards(): activ = lax.all_gather(activ_chunk, 'tp', axis=1, tiled=True)  9.24 us
    pallas_call x1, Pallas kernels, local_attention(): pl.pallas_call(attention_kernel, out_shape=jax.ShapeDtypeStruct((row_coun...  2.68 us
  transfers between devices with their start and end apart: 2, of which 2 were waited for; matrix products, arithmetic and copies ran while one was open for 4% of the time, Pallas kernels for 0%

profile of v6, /device:TPU:33, one launch (start us, length us, event | category | flops | bytes accessed | tf_op | source)
XLA Modules:
  0.0 124.8 jit_solution(15027214335879990527)
XLA Ops:
  0.0 0.0 copy-start
  0.0 0.0 copy-start.1
  0.0 0.0 copy-start.2
  0.0 0.9 constant_dynamic-slice_fusion.1
  0.9 0.1 copy.38
  1.0 0.1 iota_compare_fusion.1
  1.1 0.1 eq.65
  1.2 0.1 fusion.15
  1.3 0.2 select_reduce_fusion
  1.5 0.1 eq.69
  1.5 0.1 copy.39
  1.7 2.7 %shard_map.136 = bf16[4,576]{1,0:T(4,128)(2,1)} custom-call(s32[4]{0:T(128)} %len_ref.1, bf16[4,576]{1,0:T(4,128)(2,1)} %q_ref.1, bf16[4,576]{1,0:T(4,128)(2,1)} %nk_ref.1, bf16[4,576]{1,0:T(4,128)(2,1)} %nv_ref.1, bf16[4,576,128]{2,1,0:T(8,128)(2,1)} %bitcast.36, bf16[4,576,128]{2,1,0:T(8,128)(2,1)} %bitcast.37), custom_call_target="tpu_custom_call" | custom-call | flops 10616832 | bytes 1198080 | tf_op jit(solution)/shard_map/pallas_call | solution.py:65
  4.3 0.0 copy-done
  4.3 1.1 convolution_bitcast_fusion
  5.5 9.5 %all-gather.1 = f32[4,4,2304]{2,1,0:T(4,128)S(1)} all-gather(f32[1,4,2304]{2,1,0:T(4,128)S(1)} %convolution_bitcast_fusion), channel_id=2, replica_groups=mesh['req'=128,'tp'=4] {'tp'}, dimensions={0}, use_global_device_ids=true | all-gather | bytes 184320 | tf_op jit(solution)/shard_map/all_gather | solution.py:121
  15.0 0.0 copy-done.1
  15.0 0.1 multiply_reduce_fusion
  15.2 0.1 and_reduce_fusion
  15.3 0.0 copy-done.2
  15.3 0.2 convolution_convert_fusion.2
  15.5 0.9 broadcast_in_dim.23
  16.4 22.3 %all-to-all-start = ((bf16[128,2,576]{2,1,0:T(2,128)(2,1)}), bf16[128,2,576]{2,1,0:T(2,128)(2,1)S(1)}, u32[]{:S(2)}, u32[]{:S(2)}) async-start(bf16[128,2,576]{2,1,0:T(2,128)(2,1)} %bitcast.4), calls=%async_computation | async-start | bytes 655360 | tf_op jit(solution)/shard_map/all_to_all | solution.py:138
  38.8 1.3 %copy.41 = bf16[576,360]{0,1:T(8,128)(2,1)S(1)} copy(bf16[576,360]{1,0:T(8,128)(2,1)} %param.26) | data formatting | bytes 829440 | tf_op args[12]
  40.0 0.9 reshape.164
  41.0 1.2 %copy.40 = bf16[576,360]{0,1:T(8,128)(2,1)S(1)} copy(bf16[576,360]{1,0:T(8,128)(2,1)} %param.25) | data formatting | bytes 829440 | tf_op args[11]
  42.2 0.9 reshape.163
  43.1 21.1 %all-to-all-done = bf16[128,2,576]{2,1,0:T(2,128)(2,1)S(1)} async-done(((bf16[128,2,576]{2,1,0:T(2,128)(2,1)}), bf16[128,2,576]{2,1,0:T(2,128)(2,1)S(1)}, u32[]{:S(2)}, u32[]{:S(2)}) %all-to-all-start) | async-done | bytes 294944 | tf_op jit(solution)/shard_map/all_to_all | solution.py:138
  64.2 0.2 reshape.166
  64.4 1.7 %fusion = bf16[4,256,180]{1,2,0:T(8,128)(2,1)S(1)} fusion(bf16[576,4,90]{0,2,1:T(8,128)(2,1)} %reshape.164, bf16[576,4,90]{0,2,1:T(8,128)(2,1)} %reshape.163, bf16[256,576]{1,0:T(8,128)(2,1)S(1)} %reshape.166), kind=kOutput, calls=%fused_computation.3 | convolution fusion | flops 214179840 | bytes 1492992 | tf_op jit(solution)/shard_map/sf,ftk->tsk/dot_general | solution.py:149
  66.1 10.9 %all_to_all.15 = bf16[4,256,180]{1,2,0:T(8,128)(2,1)S(1)} all-to-all(bf16[4,256,180]{1,2,0:T(8,128)(2,1)S(1)} %fusion), channel_id=1, replica_groups=mesh['req'=128,'tp'=4] {'tp'}, dimensions={0} | all-to-all | bytes 737280 | tf_op jit(solution)/shard_map/all_to_all | solution.py:152
  77.1 9.2 %all-gather.2 = bf16[4,90,256]{2,1,0:T(8,128)(2,1)S(1)} all-gather(bf16[1,90,256]{2,1,0:T(8,128)(2,1)S(1)} %fusion.8), channel_id=1, replica_groups=mesh['req'=128,'tp'=4] {'tp'}, dimensions={0}, use_global_device_ids=true | all-gather | bytes 230400 | tf_op jit(solution)/shard_map/all_gather | solution.py:156
  86.3 0.1 reshape.173
  86.4 1.3 %convolution_convert_fusion.1 = bf16[256,576]{0,1:T(8,128)(2,1)S(1)} fusion(bf16[360,256]{1,0:T(8,128)(2,1)S(1)} %reshape.173, bf16[360,576]{0,1:T(8,128)(2,1)} %param.27), kind=kOutput, calls=%fused_computation.2 | convolution fusion | flops 106315776 | bytes 893952 | tf_op jit(solution)/shard_map/dot_general | solution.py:158
  87.7 0.2 copy.44
  87.9 0.9 reshape.167
  88.8 9.5 %all-to-all-start.2 = ((bf16[128,2,576]{2,1,0:T(2,128)(2,1)}), bf16[128,2,576]{2,1,0:T(2,128)(2,1)S(1)}, u32[]{:S(2)}, u32[]{:S(2)}) async-start(bf16[128,2,576]{2,1,0:T(2,128)(2,1)} %reshape.167), calls=%async_computation.2 | async-start | bytes 655360 | tf_op jit(solution)/shard_map/all_to_all | solution.py:162
  98.3 0.8 constant_dynamic-slice_fusion
  99.0 0.1 fusion.10
  99.1 24.6 %all-to-all-done.2 = bf16[128,2,576]{2,1,0:T(2,128)(2,1)S(1)} async-done(((bf16[128,2,576]{2,1,0:T(2,128)(2,1)}), bf16[128,2,576]{2,1,0:T(2,128)(2,1)S(1)}, u32[]{:S(2)}, u32[]{:S(2)}) %all-to-all-start.2) | async-done | bytes 294944 | tf_op jit(solution)/shard_map/all_to_all | solution.py:162
  123.6 0.3 convert_reduce_fusion.1
  123.9 0.8 fusion.2
  (7 shorter events, 0.2 us)
Async XLA Ops:
  0.0 4.3 %copy-start = (bf16[576,2304]{1,0:T(8,128)(2,1)S(1)}, bf16[576,2304]{1,0:T(8,128)(2,1)}, u32[]{:S(2)}) copy-start(bf16[576,2304]{1,0:T(8,128)(2,1)} %param.21) | copy-start | bytes 7962628
  0.0 15.0 %copy-start.1 = (bf16[4,2304]{1,0:T(4,128)(2,1)S(1)}, bf16[4,2304]{1,0:T(4,128)(2,1)}, u32[]{:S(2)}) copy-start(bf16[4,2304]{1,0:T(4,128)(2,1)} %param.20) | copy-start | bytes 55300
  0.0 15.3 %copy-start.2 = (f32[576]{0:T(1024)S(1)}, f32[576]{0:T(1024)}, u32[]{:S(2)}) copy-start(f32[576]{0:T(1024)} %param.22) | copy-start | bytes 6916
  16.4 47.8 %all-to-all-start = ((bf16[128,2,576]{2,1,0:T(2,128)(2,1)}), bf16[128,2,576]{2,1,0:T(2,128)(2,1)S(1)}, u32[]{:S(2)}, u32[]{:S(2)}) async-start(bf16[128,2,576]{2,1,0:T(2,128)(2,1)} %bitcast.4), calls=%async_computation | async-start | bytes 655360 | tf_op jit(solution)/shard_map/all_to_all | solution.py:138
  88.8 34.9 %all-to-all-start.2 = ((bf16[128,2,576]{2,1,0:T(2,128)(2,1)}), bf16[128,2,576]{2,1,0:T(2,128)(2,1)S(1)}, u32[]{:S(2)}, u32[]{:S(2)}) async-start(bf16[128,2,576]{2,1,0:T(2,128)(2,1)} %reshape.167), calls=%async_computation.2 | async-start | bytes 655360 | tf_op jit(solution)/shard_map/all_to_all | solution.py:162

commit v7 on v6

--- a/solution.py
+++ b/solution.py
@@ -138,22 +138,15 @@
     arrived = lax.all_to_all(outgoing, "req", split_axis=0, concat_axis=0, tiled=True)
     token_rows = arrived.reshape(req_count * capacity, share)
     tp_count = lax.axis_size("tp")
-    chunk = gate_weight.shape[1] // tp_count
-    paired_weight = jnp.concatenate(
-        [
-            gate_weight.reshape(share, tp_count, chunk),
-            up_weight.reshape(share, tp_count, chunk),
-        ],
-        axis=2,
+    paired_weight = jnp.concatenate([gate_weight, up_weight], axis=1)
+    both = jnp.dot(token_rows, paired_weight, preferred_element_type=jnp.float32).astype(
+        jnp.bfloat16
     )
-    both = jnp.einsum(
-        "sf,ftk->tsk", token_rows, paired_weight, preferred_element_type=jnp.float32
-    ).astype(jnp.bfloat16)
+    both = jnp.broadcast_to(both[None], (tp_count,) + both.shape)
     both = lax.all_to_all(both, "tp", split_axis=0, concat_axis=0, tiled=True)
     summed = jnp.sum(both.astype(jnp.float32), axis=0)
-    summed = jnp.stack([summed[:, :chunk], summed[:, chunk:]], axis=1)
-    activ_chunk = (jax.nn.silu(summed[:, 0]) * summed[:, 1]).astype(jnp.bfloat16)
-    activ = lax.all_gather(activ_chunk, "tp", axis=1, tiled=True)
+    hidden_units = gate_weight.shape[1]
+    activ = (jax.nn.silu(summed[:, :hidden_units]) * summed[:, hidden_units:]).astype(jnp.bfloat16)
     partial_out = (
         jnp.dot(activ, down_weight, preferred_element_type=jnp.float32)
         .astype(jnp.bfloat16)

time: 125 us -> 124 us (level)
  blocking collectives: 29.6 us -> 79.5 us
  starting transfers between devices: 31.8 us -> 6.78 us
  waiting for transfers between devices: 45.6 us -> 24.6 us
  local copies, waits for them, and re-layouts: 8.64 us -> 4.41 us
    all_to_all x0 -> x1, blocking collectives: none -> 47.5 us  [shards(): lax.all_to_all(outgoing, 'req', split_axis=0, concat_axis=0, tiled=True)]
    all_to_all x1 -> x0, starting transfers between devices: 22.3 us -> none  [shards(): lax.all_to_all(outgoing, 'req', split_axis=0, concat_axis=0, tiled=True)]
    all_to_all x1 -> x0, waiting for transfers between devices: 21.1 us -> none  [shards(): lax.all_to_all(outgoing, 'req', split_axis=0, concat_axis=0, tiled=True)]
    all_to_all x1, blocking collectives: 10.9 us -> 22.4 us  [shards(): both = lax.all_to_all(both, 'tp', split_axis=0, concat_axis=0, tiled=True)]
    all_gather x1 -> x0, blocking collectives: 9.24 us -> none  [shards(): activ = lax.all_gather(activ_chunk, 'tp', axis=1, tiled=True)]
    all_to_all x1, starting transfers between devices: 9.46 us -> 6.78 us  [shards(): lax.all_to_all(partial_out, 'req', split_axis=0, concat_axis=0, tiled=True)]
    reshape x2 -> x0, local copies, waits for them, and re-layouts: 1.83 us -> none  [the longest x1 0.92 us: shards(): gate_weight.reshape(share, tp_count, chunk)]
    unnamed x9 -> x8, local copies, waits for them, and re-layouts: 2.57 us -> 0.8 us
  transfers between devices with their start and end apart: 2 -> 1, of which waited for: 2 -> 1; matrix products, arithmetic and copies ran while one was open for 4% -> 1% of each run, Pallas kernels for 0% -> 0%
where the time goes in v7:
time: 124 us
  blocking collectives  79.5 us (64%)
  waiting for transfers between devices  24.6 us (20%)
  starting transfers between devices  6.78 us (5%)
  matrix products  4.68 us (4%)
  local copies, waits for them, and re-layouts  4.41 us (4%)
  Pallas kernels  2.68 us (2%)
    all_to_all x1, blocking collectives, shards(): lax.all_to_all(outgoing, 'req', split_axis=0, concat_axis=0, tiled=True)  47.5 us
    all_to_all x1, waiting for transfers between devices, shards(): lax.all_to_all(partial_out, 'req', split_axis=0, concat_axis=0, tiled=True)  24.6 us
    all_to_all x1, blocking collectives, shards(): both = lax.all_to_all(both, 'tp', split_axis=0, concat_axis=0, tiled=True)  22.4 us
    all_gather x1, blocking collectives, shards(): proj_all = lax.all_gather(proj_part, 'tp', axis=0, tiled=False)  9.52 us
    all_to_all x1, starting transfers between devices, shards(): lax.all_to_all(partial_out, 'req', split_axis=0, concat_axis=0, tiled=True)  6.78 us
    pallas_call x1, Pallas kernels, local_attention(): pl.pallas_call(attention_kernel, out_shape=jax.ShapeDtypeStruct((row_coun...  2.68 us
  transfers between devices with their start and end apart: 1, of which 1 were waited for; matrix products, arithmetic and copies ran while one was open for 1% of the time, Pallas kernels for 0%

profile of v7, /device:TPU:33, one launch (start us, length us, event | category | flops | bytes accessed | tf_op | source)
XLA Modules:
  0.0 123.9 jit_solution(2637505392325675321)
XLA Ops:
  0.0 0.0 copy-start
  0.0 0.9 constant_dynamic-slice_fusion.1
  0.9 0.1 copy.38
  1.0 0.1 iota_compare_fusion.1
  1.1 0.1 eq.65
  1.2 0.1 fusion.14
  1.3 0.2 select_reduce_fusion
  1.4 0.1 eq.69
  1.5 0.1 copy.39
  1.6 2.7 %shard_map.136 = bf16[4,576]{1,0:T(4,128)(2,1)} custom-call(s32[4]{0:T(128)} %len_ref.1, bf16[4,576]{1,0:T(4,128)(2,1)} %q_ref.1, bf16[4,576]{1,0:T(4,128)(2,1)} %nk_ref.1, bf16[4,576]{1,0:T(4,128)(2,1)} %nv_ref.1, bf16[4,576,128]{2,1,0:T(8,128)(2,1)} %bitcast.24, bf16[4,576,128]{2,1,0:T(8,128)(2,1)} %bitcast.25), custom_call_target="tpu_custom_call" | custom-call | flops 10616832 | bytes 1198080 | tf_op jit(solution)/shard_map/pallas_call | solution.py:65
  4.3 0.0 copy-done
  4.3 0.0 copy-start.1
  4.3 0.0 copy-start.3
  4.3 1.2 convolution_bitcast_fusion
  5.5 9.5 %all-gather.1 = f32[4,4,2304]{2,1,0:T(4,128)S(1)} all-gather(f32[1,4,2304]{2,1,0:T(4,128)S(1)} %convolution_bitcast_fusion), channel_id=2, replica_groups=mesh['req'=128,'tp'=4] {'tp'}, dimensions={0}, use_global_device_ids=true | all-gather | bytes 184320 | tf_op jit(solution)/shard_map/all_gather | solution.py:121
  15.0 0.0 copy-done.1
  15.1 0.1 multiply_reduce_fusion
  15.2 0.1 and_reduce_fusion
  15.3 0.0 copy-done.3
  15.3 0.2 convolution_convert_fusion.2
  15.5 0.2 broadcast_in_dim.18
  15.7 47.5 %all_to_all.15 = bf16[128,2,576]{2,1,0:T(2,128)(2,1)S(1)} all-to-all(bf16[128,2,576]{2,1,0:T(2,128)(2,1)S(1)} %bitcast.23), channel_id=1, replica_groups=mesh['req'=128,'tp'=4] {'req'}, dimensions={0} | all-to-all | bytes 589824 | tf_op jit(solution)/shard_map/all_to_all | solution.py:138
  63.3 0.2 reshape.159
  63.5 2.1 %convolution_convert_fusion = bf16[256,720]{0,1:T(8,128)(2,1)S(1)} fusion(bf16[256,576]{1,0:T(8,128)(2,1)S(1)} %reshape.159, bf16[576,360]{1,0:T(8,128)(2,1)} %param.26, bf16[576,360]{1,0:T(8,128)(2,1)} %param.25), kind=kOutput, calls=%fused_computation.2 | convolution fusion | flops 214179840 | bytes 1492992 | tf_op jit(solution)/shard_map/dot_general | solution.py:142
  65.6 0.1 broadcast_in_dim.30
  65.7 22.4 %all_to_all.16 = bf16[4,256,720]{1,2,0:T(8,128)(2,1)S(1)} all-to-all(bf16[4,256,720]{1,2,0:T(8,128)(2,1)S(1)} %broadcast_in_dim.30), channel_id=1, replica_groups=mesh['req'=128,'tp'=4] {'tp'}, dimensions={0} | all-to-all | bytes 2949120 | tf_op jit(solution)/shard_map/all_to_all | solution.py:146
  88.1 0.0 copy-start.2
  88.1 0.2 convert_reduce_fusion
  88.4 0.8 copy-done.2
  89.2 0.4 convolution_convert_fusion.1
  89.5 0.2 copy.41
  89.8 0.9 reshape.160
  90.6 6.8 %all-to-all-start.2 = ((bf16[128,2,576]{2,1,0:T(2,128)(2,1)}), bf16[128,2,576]{2,1,0:T(2,128)(2,1)S(1)}, u32[]{:S(2)}, u32[]{:S(2)}) async-start(bf16[128,2,576]{2,1,0:T(2,128)(2,1)} %reshape.160), calls=%async_computation.2 | async-start | bytes 655360 | tf_op jit(solution)/shard_map/all_to_all | solution.py:155
  97.4 0.8 constant_dynamic-slice_fusion
  98.2 0.1 fusion.9
  98.2 24.6 %all-to-all-done.2 = bf16[128,2,576]{2,1,0:T(2,128)(2,1)S(1)} async-done(((bf16[128,2,576]{2,1,0:T(2,128)(2,1)}), bf16[128,2,576]{2,1,0:T(2,128)(2,1)S(1)}, u32[]{:S(2)}, u32[]{:S(2)}) %all-to-all-start.2) | async-done | bytes 294944 | tf_op jit(solution)/shard_map/all_to_all | solution.py:155
  122.8 0.3 convert_reduce_fusion.1
  123.1 0.8 fusion.1
  (5 shorter events, 0.1 us)
Async XLA Ops:
  0.0 4.3 %copy-start = (bf16[576,2304]{1,0:T(8,128)(2,1)S(1)}, bf16[576,2304]{1,0:T(8,128)(2,1)}, u32[]{:S(2)}) copy-start(bf16[576,2304]{1,0:T(8,128)(2,1)} %param.21) | copy-start | bytes 7962628
  4.3 10.7 %copy-start.1 = (bf16[4,2304]{1,0:T(4,128)(2,1)S(1)}, bf16[4,2304]{1,0:T(4,128)(2,1)}, u32[]{:S(2)}) copy-start(bf16[4,2304]{1,0:T(4,128)(2,1)} %param.20) | copy-start | bytes 55300
  4.3 11.0 %copy-start.3 = (f32[576]{0:T(1024)S(1)}, f32[576]{0:T(1024)}, u32[]{:S(2)}) copy-start(f32[576]{0:T(1024)} %param.22) | copy-start | bytes 6916
  88.1 1.0 copy-start.2
  90.6 32.2 %all-to-all-start.2 = ((bf16[128,2,576]{2,1,0:T(2,128)(2,1)}), bf16[128,2,576]{2,1,0:T(2,128)(2,1)S(1)}, u32[]{:S(2)}, u32[]{:S(2)}) async-start(bf16[128,2,576]{2,1,0:T(2,128)(2,1)} %reshape.160), calls=%async_computation.2 | async-start | bytes 655360 | tf_op jit(solution)/shard_map/all_to_all | solution.py:155

commit v8 on v7

--- a/solution.py
+++ b/solution.py
@@ -9,7 +9,9 @@
 EXPERTS = 8
 
 
-def attention_kernel(len_ref, q_ref, nk_ref, nv_ref, k_ref, v_ref, o_ref):
+def attention_kernel(len_ref, q_ref, nk_ref, nv_ref, k_ref, v_ref, w_hbm, o_ref, attn_ref, w_ref, w_sem):
+    weight_copy = pltpu.make_async_copy(w_hbm, w_ref, w_sem)
+    weight_copy.start()
     row_count, local_width = q_ref.shape
     head_count = local_width // HD
     cache_len = k_ref.shape[2]
@@ -55,22 +57,29 @@
         rows = slice(r * head_count, (r + 1) * head_count)
         mixed = jnp.sum(mixed_heads[rows], axis=0, keepdims=True)
         own = jnp.sum(own_lanes[rows], axis=0, keepdims=True)
-        o_ref[r : r + 1, :] = (mixed + own * new_values[r : r + 1, :]).astype(o_ref.dtype)
+        attn_ref[r : r + 1, :] = (mixed + own * new_values[r : r + 1, :]).astype(attn_ref.dtype)
+    weight_copy.wait()
+    o_ref[...] = jnp.dot(attn_ref[...], w_ref[...], preferred_element_type=jnp.float32)
 
 
-def local_attention(query, new_key, new_value, key_cache, value_cache, lengths):
+def local_attention(query, new_key, new_value, key_cache, value_cache, lengths, out_weight):
     row_count, local_width = query.shape
     cache_len = key_cache.shape[1]
     vmem = pl.BlockSpec(memory_space=pltpu.VMEM)
     return pl.pallas_call(
         attention_kernel,
-        out_shape=jax.ShapeDtypeStruct((row_count, local_width), jnp.bfloat16),
-        in_specs=[pl.BlockSpec(memory_space=pltpu.SMEM)] + [vmem] * 5,
+        out_shape=jax.ShapeDtypeStruct((row_count, out_weight.shape[1]), jnp.float32),
+        in_specs=[pl.BlockSpec(memory_space=pltpu.SMEM)] + [vmem] * 5 + [pl.BlockSpec(memory_space=pl.ANY)],
         out_specs=vmem,
+        scratch_shapes=[
+            pltpu.VMEM((row_count, local_width), jnp.bfloat16),
+            pltpu.VMEM(out_weight.shape, out_weight.dtype),
+            pltpu.SemaphoreType.DMA(()),
+        ],
         cost_estimate=pl.CostEstimate(
             flops=4 * row_count * (local_width // HD) * cache_len * local_width,
             transcendentals=row_count * (local_width // HD) * (cache_len + 1),
-            bytes_accessed=2 * key_cache.size * 2 + 4 * query.size * 2,
+            bytes_accessed=2 * key_cache.size * 2 + 4 * query.size * 2 + out_weight.size * 2,
         ),
     )(
         lengths,
@@ -79,6 +88,7 @@
         new_value,
         jnp.swapaxes(key_cache, 1, 2),
         jnp.swapaxes(value_cache, 1, 2),
+        out_weight,
     )
 
 
@@ -112,12 +122,13 @@
     down_weight,
 ):
     row_count = query.shape[0]
-    attn_out = local_attention(query, new_key, new_value, key_cache, value_cache, lengths)
+    proj_part = local_attention(
+        query, new_key, new_value, key_cache, value_cache, lengths, out_weight
+    )
     model_width = out_weight.shape[1]
     share = model_width // lax.axis_size("tp")
     col_start = lax.axis_index("tp") * share
     resid_float = resid.astype(jnp.float32)
-    proj_part = jnp.dot(attn_out, out_weight, preferred_element_type=jnp.float32)
     proj_all = lax.all_gather(proj_part, "tp", axis=0, tiled=False)
     hidden_full = resid_float + jnp.sum(proj_all, axis=0)
     mean_square = jnp.mean(hidden_full * hidden_full, axis=1)

time: 124 us -> 123 us (level)
  matrix products: 4.68 us -> 2.38 us
  Pallas kernels: 2.68 us -> 4.2 us
    pallas_call x1, Pallas kernels: 2.68 us -> 4.2 us  [local_attention(): pl.pallas_call(attention_kernel, out_shape=jax.ShapeDtypeStruct((row_coun...]
where the time goes in v8:
time: 123 us
  blocking collectives  79.8 us (65%)
  waiting for transfers between devices  24.6 us (20%)
  starting transfers between devices  6.77 us (6%)
  Pallas kernels  4.2 us (3%)
  local copies, waits for them, and re-layouts  3.54 us (3%)
  matrix products  2.38 us (2%)
    all_to_all x1, blocking collectives, shards(): lax.all_to_all(outgoing, 'req', split_axis=0, concat_axis=0, tiled=True)  47.5 us
    all_to_all x1, waiting for transfers between devices, shards(): lax.all_to_all(partial_out, 'req', split_axis=0, concat_axis=0, tiled=True)  24.6 us
    all_to_all x1, blocking collectives, shards(): both = lax.all_to_all(both, 'tp', split_axis=0, concat_axis=0, tiled=True)  22.4 us
    all_gather x1, blocking collectives, shards(): proj_all = lax.all_gather(proj_part, 'tp', axis=0, tiled=False)  9.86 us
    all_to_all x1, starting transfers between devices, shards(): lax.all_to_all(partial_out, 'req', split_axis=0, concat_axis=0, tiled=True)  6.77 us
    pallas_call x1, Pallas kernels, local_attention(): pl.pallas_call(attention_kernel, out_shape=jax.ShapeDtypeStruct((row_coun...  4.2 us
  transfers between devices with their start and end apart: 1, of which 1 were waited for; matrix products, arithmetic and copies ran while one was open for 1% of the time, Pallas kernels for 0%

profile of v8, /device:TPU:33, one launch (start us, length us, event | category | flops | bytes accessed | tf_op | source)
XLA Modules:
  0.0 122.7 jit_solution(3388109408338282826)
XLA Ops:
  0.0 0.0 copy-start
  0.0 0.8 constant_dynamic-slice_fusion.1
  0.8 0.1 copy.38
  0.9 0.1 iota_compare_fusion.1
  1.0 0.1 eq.65
  1.1 0.1 fusion.14
  1.2 0.2 select_reduce_fusion
  1.3 0.1 eq.69
  1.4 0.1 copy.39
  1.5 0.0 copy-start.1
  1.5 0.0 copy-start.4
  1.6 4.2 %shard_map.136 = f32[4,2304]{1,0:T(4,128)} custom-call(s32[4]{0:T(128)} %len_ref.1, bf16[4,576]{1,0:T(4,128)(2,1)} %q_ref.1, bf16[4,576]{1,0:T(4,128)(2,1)} %nk_ref.1, bf16[4,576]{1,0:T(4,128)(2,1)} %nv_ref.1, bf16[4,576,128]{2,1,0:T(8,128)(2,1)} %bitcast.21, bf16[4,576,128]{2,1,0:T(8,128)(2,1)} %bitcast.22, bf16[576,2304]{1,0:T(8,128)(2,1)} %w_hbm.1), custom_call_target="tpu_custom_call" | custom-call | flops 10616832 | bytes 3852288 | tf_op jit(solution)/shard_map/pallas_call | solution.py:69
  5.8 0.0 copy-start.2
  5.8 0.0 copy-start.3
  5.8 9.9 %all-gather.1 = f32[4,4,2304]{2,1,0:T(4,128)S(1)} all-gather(f32[1,4,2304]{2,1,0:T(4,128)} %bitcast.23), channel_id=2, replica_groups=mesh['req'=128,'tp'=4] {'tp'}, dimensions={0}, use_global_device_ids=true | all-gather | bytes 184320 | tf_op jit(solution)/shard_map/all_gather | solution.py:132
  15.7 0.0 copy-done.1
  15.7 0.1 multiply_reduce_fusion
  15.8 0.1 and_reduce_fusion
  15.9 0.0 copy-done.4
  15.9 0.2 convolution_convert_fusion.2
  16.2 0.2 broadcast_in_dim.18
  16.4 47.5 %all_to_all.15 = bf16[128,2,576]{2,1,0:T(2,128)(2,1)S(1)} all-to-all(bf16[128,2,576]{2,1,0:T(2,128)(2,1)S(1)} %bitcast.20), channel_id=1, replica_groups=mesh['req'=128,'tp'=4] {'req'}, dimensions={0} | all-to-all | bytes 589824 | tf_op jit(solution)/shard_map/all_to_all | solution.py:149
  63.9 0.2 reshape.159
  64.2 0.0 copy-done.2
  64.2 0.0 copy-done.3
  64.2 0.9 convolution_convert_fusion
  65.1 0.1 broadcast_in_dim.30
  65.2 22.4 %all_to_all.16 = bf16[4,256,720]{1,2,0:T(8,128)(2,1)S(1)} all-to-all(bf16[4,256,720]{1,2,0:T(8,128)(2,1)S(1)} %broadcast_in_dim.30), channel_id=1, replica_groups=mesh['req'=128,'tp'=4] {'tp'}, dimensions={0} | all-to-all | bytes 2949120 | tf_op jit(solution)/shard_map/all_to_all | solution.py:157
  87.7 0.2 convert_reduce_fusion
  87.9 0.0 copy-done
  87.9 0.4 convolution_convert_fusion.1
  88.3 0.2 copy.41
  88.5 0.9 reshape.160
  89.4 6.8 %all-to-all-start.2 = ((bf16[128,2,576]{2,1,0:T(2,128)(2,1)}), bf16[128,2,576]{2,1,0:T(2,128)(2,1)S(1)}, u32[]{:S(2)}, u32[]{:S(2)}) async-start(bf16[128,2,576]{2,1,0:T(2,128)(2,1)} %reshape.160), calls=%async_computation.2 | async-start | bytes 655360 | tf_op jit(solution)/shard_map/all_to_all | solution.py:166
  96.1 0.8 constant_dynamic-slice_fusion
  96.9 0.1 fusion.9
  97.0 24.6 %all-to-all-done.2 = bf16[128,2,576]{2,1,0:T(2,128)(2,1)S(1)} async-done(((bf16[128,2,576]{2,1,0:T(2,128)(2,1)}), bf16[128,2,576]{2,1,0:T(2,128)(2,1)S(1)}, u32[]{:S(2)}, u32[]{:S(2)}) %all-to-all-start.2) | async-done | bytes 294944 | tf_op jit(solution)/shard_map/all_to_all | solution.py:166
  121.5 0.3 convert_reduce_fusion.1
  121.8 0.8 fusion.1
  (5 shorter events, 0.1 us)
Async XLA Ops:
  0.0 87.9 %copy-start = (bf16[360,576]{0,1:T(8,128)(2,1)S(1)}, bf16[360,576]{0,1:T(8,128)(2,1)}, u32[]{:S(2)}) copy-start(bf16[360,576]{0,1:T(8,128)(2,1)} %param.27) | copy-start | bytes 1244164
  1.5 14.1 %copy-start.1 = (bf16[4,2304]{1,0:T(4,128)(2,1)S(1)}, bf16[4,2304]{1,0:T(4,128)(2,1)}, u32[]{:S(2)}) copy-start(bf16[4,2304]{1,0:T(4,128)(2,1)} %param.20) | copy-start | bytes 55300
  1.5 14.4 %copy-start.4 = (f32[576]{0:T(1024)S(1)}, f32[576]{0:T(1024)}, u32[]{:S(2)}) copy-start(f32[576]{0:T(1024)} %param.22) | copy-start | bytes 6916
  5.8 58.4 %copy-start.2 = (bf16[576,360]{1,0:T(8,128)(2,1)S(1)}, bf16[576,360]{1,0:T(8,128)(2,1)}, u32[]{:S(2)}) copy-start(bf16[576,360]{1,0:T(8,128)(2,1)} %param.26) | copy-start | bytes 1244164
  5.8 58.4 %copy-start.3 = (bf16[576,360]{1,0:T(8,128)(2,1)S(1)}, bf16[576,360]{1,0:T(8,128)(2,1)}, u32[]{:S(2)}) copy-start(bf16[576,360]{1,0:T(8,128)(2,1)} %param.25) | copy-start | bytes 1244164
  89.4 32.2 %all-to-all-start.2 = ((bf16[128,2,576]{2,1,0:T(2,128)(2,1)}), bf16[128,2,576]{2,1,0:T(2,128)(2,1)S(1)}, u32[]{:S(2)}, u32[]{:S(2)}) async-start(bf16[128,2,576]{2,1,0:T(2,128)(2,1)} %reshape.160), calls=%async_computation.2 | async-start | bytes 655360 | tf_op jit(solution)/shard_map/all_to_all | solution.py:166

commit v9 on v8

--- a/solution.py
+++ b/solution.py
@@ -10,8 +10,16 @@
 
 
 def attention_kernel(len_ref, q_ref, nk_ref, nv_ref, k_ref, v_ref, w_hbm, o_ref, attn_ref, w_ref, w_sem):
-    weight_copy = pltpu.make_async_copy(w_hbm, w_ref, w_sem)
-    weight_copy.start()
+    pieces = w_sem.shape[0]
+    piece = w_ref.shape[0] // pieces
+    weight_copies = [
+        pltpu.make_async_copy(
+            w_hbm.at[pl.ds(p * piece, piece)], w_ref.at[pl.ds(p * piece, piece)], w_sem.at[p]
+        )
+        for p in range(pieces)
+    ]
+    for weight_copy in weight_copies:
+        weight_copy.start()
     row_count, local_width = q_ref.shape
     head_count = local_width // HD
     cache_len = k_ref.shape[2]
@@ -58,8 +66,17 @@
         mixed = jnp.sum(mixed_heads[rows], axis=0, keepdims=True)
         own = jnp.sum(own_lanes[rows], axis=0, keepdims=True)
         attn_ref[r : r + 1, :] = (mixed + own * new_values[r : r + 1, :]).astype(attn_ref.dtype)
-    weight_copy.wait()
-    o_ref[...] = jnp.dot(attn_ref[...], w_ref[...], preferred_element_type=jnp.float32)
+    attn = attn_ref[...]
+    total = None
+    for p, weight_copy in enumerate(weight_copies):
+        weight_copy.wait()
+        part = jnp.dot(
+            attn[:, p * piece : (p + 1) * piece],
+            w_ref[p * piece : (p + 1) * piece, :],
+            preferred_element_type=jnp.float32,
+        )
+        total = part if total is None else total + part
+    o_ref[...] = total
 
 
 def local_attention(query, new_key, new_value, key_cache, value_cache, lengths, out_weight):
@@ -74,7 +91,7 @@
         scratch_shapes=[
             pltpu.VMEM((row_count, local_width), jnp.bfloat16),
             pltpu.VMEM(out_weight.shape, out_weight.dtype),
-            pltpu.SemaphoreType.DMA(()),
+            pltpu.SemaphoreType.DMA((4,)),
         ],
         cost_estimate=pl.CostEstimate(
             flops=4 * row_count * (local_width // HD) * cache_len * local_width,

time: 123 us -> 123 us (level)
  no operation moved by 1% of the time
where the time goes in v9:
time: 123 us; the launch traced here: 122 us
  blocking collectives  79.8 us (65%)
  waiting for transfers between devices  24.6 us (20%)
  starting transfers between devices  6.77 us (6%)
  Pallas kernels  3.92 us (3%)
  local copies, waits for them, and re-layouts  3.54 us (3%)
  matrix products  2.38 us (2%)
    all_to_all x1, blocking collectives, shards(): lax.all_to_all(outgoing, 'req', split_axis=0, concat_axis=0, tiled=True)  47.5 us
    all_to_all x1, waiting for transfers between devices, shards(): lax.all_to_all(partial_out, 'req', split_axis=0, concat_axis=0, tiled=True)  24.6 us
    all_to_all x1, blocking collectives, shards(): both = lax.all_to_all(both, 'tp', split_axis=0, concat_axis=0, tiled=True)  22.4 us
    all_gather x1, blocking collectives, shards(): proj_all = lax.all_gather(proj_part, 'tp', axis=0, tiled=False)  9.86 us
    all_to_all x1, starting transfers between devices, shards(): lax.all_to_all(partial_out, 'req', split_axis=0, concat_axis=0, tiled=True)  6.77 us
    pallas_call x1, Pallas kernels, local_attention(): pl.pallas_call(attention_kernel, out_shape=jax.ShapeDtypeStruct((row_coun...  3.92 us
  transfers between devices with their start and end apart: 1, of which 1 were waited for; matrix products, arithmetic and copies ran while one was open for 1% of the time, Pallas kernels for 0%

profile of v9, /device:TPU:33, one launch (start us, length us, event | category | flops | bytes accessed | tf_op | source)
XLA Modules:
  0.0 122.4 jit_solution(5806786700422963009)
XLA Ops:
  0.0 0.0 copy-start
  0.0 0.8 constant_dynamic-slice_fusion.1
  0.8 0.1 copy.38
  0.9 0.1 iota_compare_fusion.1
  1.0 0.1 eq.65
  1.1 0.1 fusion.14
  1.2 0.2 select_reduce_fusion
  1.3 0.1 eq.69
  1.4 0.1 copy.39
  1.5 0.0 copy-start.1
  1.5 0.0 copy-start.4
  1.6 3.9 %shard_map.136 = f32[4,2304]{1,0:T(4,128)} custom-call(s32[4]{0:T(128)} %len_ref.1, bf16[4,576]{1,0:T(4,128)(2,1)} %q_ref.1, bf16[4,576]{1,0:T(4,128)(2,1)} %nk_ref.1, bf16[4,576]{1,0:T(4,128)(2,1)} %nv_ref.1, bf16[4,576,128]{2,1,0:T(8,128)(2,1)} %bitcast.21, bf16[4,576,128]{2,1,0:T(8,128)(2,1)} %bitcast.22, bf16[576,2304]{1,0:T(8,128)(2,1)} %w_hbm.1), custom_call_target="tpu_custom_call" | custom-call | flops 10616832 | bytes 3852288 | tf_op jit(solution)/shard_map/pallas_call | solution.py:86
  5.5 0.0 copy-start.2
  5.5 0.0 copy-start.3
  5.5 9.9 %all-gather.1 = f32[4,4,2304]{2,1,0:T(4,128)S(1)} all-gather(f32[1,4,2304]{2,1,0:T(4,128)} %bitcast.23), channel_id=2, replica_groups=mesh['req'=128,'tp'=4] {'tp'}, dimensions={0}, use_global_device_ids=true | all-gather | bytes 184320 | tf_op jit(solution)/shard_map/all_gather | solution.py:149
  15.4 0.0 copy-done.1
  15.4 0.1 multiply_reduce_fusion
  15.6 0.1 and_reduce_fusion
  15.6 0.0 copy-done.4
  15.7 0.2 convolution_convert_fusion.2
  15.9 0.2 broadcast_in_dim.18
  16.1 47.5 %all_to_all.15 = bf16[128,2,576]{2,1,0:T(2,128)(2,1)S(1)} all-to-all(bf16[128,2,576]{2,1,0:T(2,128)(2,1)S(1)} %bitcast.20), channel_id=1, replica_groups=mesh['req'=128,'tp'=4] {'req'}, dimensions={0} | all-to-all | bytes 589824 | tf_op jit(solution)/shard_map/all_to_all | solution.py:166
  63.6 0.2 reshape.159
  63.9 0.0 copy-done.2
  63.9 0.0 copy-done.3
  63.9 0.9 convolution_convert_fusion
  64.8 0.1 broadcast_in_dim.30
  64.9 22.4 %all_to_all.16 = bf16[4,256,720]{1,2,0:T(8,128)(2,1)S(1)} all-to-all(bf16[4,256,720]{1,2,0:T(8,128)(2,1)S(1)} %broadcast_in_dim.30), channel_id=1, replica_groups=mesh['req'=128,'tp'=4] {'tp'}, dimensions={0} | all-to-all | bytes 2949120 | tf_op jit(solution)/shard_map/all_to_all | solution.py:174
  87.4 0.2 convert_reduce_fusion
  87.6 0.0 copy-done
  87.6 0.4 convolution_convert_fusion.1
  88.0 0.2 copy.41
  88.2 0.9 reshape.160
  89.1 6.8 %all-to-all-start.2 = ((bf16[128,2,576]{2,1,0:T(2,128)(2,1)}), bf16[128,2,576]{2,1,0:T(2,128)(2,1)S(1)}, u32[]{:S(2)}, u32[]{:S(2)}) async-start(bf16[128,2,576]{2,1,0:T(2,128)(2,1)} %reshape.160), calls=%async_computation.2 | async-start | bytes 655360 | tf_op jit(solution)/shard_map/all_to_all | solution.py:183
  95.9 0.8 constant_dynamic-slice_fusion
  96.6 0.1 fusion.9
  96.7 24.6 %all-to-all-done.2 = bf16[128,2,576]{2,1,0:T(2,128)(2,1)S(1)} async-done(((bf16[128,2,576]{2,1,0:T(2,128)(2,1)}), bf16[128,2,576]{2,1,0:T(2,128)(2,1)S(1)}, u32[]{:S(2)}, u32[]{:S(2)}) %all-to-all-start.2) | async-done | bytes 294944 | tf_op jit(solution)/shard_map/all_to_all | solution.py:183
  121.3 0.3 convert_reduce_fusion.1
  121.5 0.8 fusion.1
  (5 shorter events, 0.1 us)
Async XLA Ops:
  0.0 87.6 %copy-start = (bf16[360,576]{0,1:T(8,128)(2,1)S(1)}, bf16[360,576]{0,1:T(8,128)(2,1)}, u32[]{:S(2)}) copy-start(bf16[360,576]{0,1:T(8,128)(2,1)} %param.27) | copy-start | bytes 1244164
  1.5 13.9 %copy-start.1 = (bf16[4,2304]{1,0:T(4,128)(2,1)S(1)}, bf16[4,2304]{1,0:T(4,128)(2,1)}, u32[]{:S(2)}) copy-start(bf16[4,2304]{1,0:T(4,128)(2,1)} %param.20) | copy-start | bytes 55300
  1.5 14.1 %copy-start.4 = (f32[576]{0:T(1024)S(1)}, f32[576]{0:T(1024)}, u32[]{:S(2)}) copy-start(f32[576]{0:T(1024)} %param.22) | copy-start | bytes 6916
  5.5 58.4 %copy-start.2 = (bf16[576,360]{1,0:T(8,128)(2,1)S(1)}, bf16[576,360]{1,0:T(8,128)(2,1)}, u32[]{:S(2)}) copy-start(bf16[576,360]{1,0:T(8,128)(2,1)} %param.26) | copy-start | bytes 1244164
  5.5 58.4 %copy-start.3 = (bf16[576,360]{1,0:T(8,128)(2,1)S(1)}, bf16[576,360]{1,0:T(8,128)(2,1)}, u32[]{:S(2)}) copy-start(bf16[576,360]{1,0:T(8,128)(2,1)} %param.25) | copy-start | bytes 1244164
  89.1 32.2 %all-to-all-start.2 = ((bf16[128,2,576]{2,1,0:T(2,128)(2,1)}), bf16[128,2,576]{2,1,0:T(2,128)(2,1)S(1)}, u32[]{:S(2)}, u32[]{:S(2)}) async-start(bf16[128,2,576]{2,1,0:T(2,128)(2,1)} %reshape.160), calls=%async_computation.2 | async-start | bytes 655360 | tf_op jit(solution)/shard_map/all_to_all | solution.py:183

commit v10 on v9

--- a/solution.py
+++ b/solution.py
@@ -146,7 +146,14 @@
     share = model_width // lax.axis_size("tp")
     col_start = lax.axis_index("tp") * share
     resid_float = resid.astype(jnp.float32)
-    proj_all = lax.all_gather(proj_part, "tp", axis=0, tiled=False)
+    tp_count = lax.axis_size("tp")
+    proj_all = lax.all_to_all(
+        jnp.broadcast_to(proj_part[None], (tp_count,) + proj_part.shape),
+        "tp",
+        split_axis=0,
+        concat_axis=0,
+        tiled=True,
+    )
     hidden_full = resid_float + jnp.sum(proj_all, axis=0)
     mean_square = jnp.mean(hidden_full * hidden_full, axis=1)
     inv_rms = lax.rsqrt(mean_square + 1e-05)
@@ -165,7 +172,6 @@
     outgoing = jnp.repeat(expert_rows, group_size, axis=0)
     arrived = lax.all_to_all(outgoing, "req", split_axis=0, concat_axis=0, tiled=True)
     token_rows = arrived.reshape(req_count * capacity, share)
-    tp_count = lax.axis_size("tp")
     paired_weight = jnp.concatenate([gate_weight, up_weight], axis=1)
     both = jnp.dot(token_rows, paired_weight, preferred_element_type=jnp.float32).astype(
         jnp.bfloat16

time: 123 us -> 120 us (0.976)
  blocking collectives: 79.8 us -> 68.3 us
  starting transfers between devices: 6.77 us -> 10.3 us
  waiting for transfers between devices: 24.6 us -> 27.9 us
  local copies, waits for them, and re-layouts: 3.54 us -> 5 us
    all_gather x1 -> x0, blocking collectives: 9.86 us -> none  [shards(): proj_all = lax.all_gather(proj_part, 'tp', axis=0, tiled=False)]
    all_to_all x0 -> x1, starting transfers between devices: none -> 4.01 us  [shards(): lax.all_to_all(jnp.broadcast_to(proj_part[None], (tp_count,) + proj_part....]
    all_to_all x0 -> x1, waiting for transfers between devices: none -> 3.34 us  [shards(): lax.all_to_all(jnp.broadcast_to(proj_part[None], (tp_count,) + proj_part....]
    broadcast_in_dim x0 -> x1, local copies, waits for them, and re-layouts: none -> 1.52 us  [shards(): jnp.broadcast_to(proj_part[None], (tp_count,) + proj_part.shape)]
    all_to_all x1, blocking collectives: 47.5 us -> 46.1 us  [shards(): lax.all_to_all(outgoing, 'req', split_axis=0, concat_axis=0, tiled=True)]
  transfers between devices with their start and end apart: 1 -> 2, of which waited for: 1 -> 2; matrix products, arithmetic and copies ran while one was open for 1% -> 2% of each run, Pallas kernels for 0% -> 0%
where the time goes in v10:
time: 120 us; the launch traced here: 119 us
  blocking collectives  68.3 us (57%)
  waiting for transfers between devices  27.9 us (23%)
  starting transfers between devices  10.3 us (9%)
  local copies, waits for them, and re-layouts  5 us (4%)
  Pallas kernels  3.95 us (3%)
  matrix products  2.38 us (2%)
  other arithmetic  1.22 us (1%)
    all_to_all x1, blocking collectives, shards(): lax.all_to_all(outgoing, 'req', split_axis=0, concat_axis=0, tiled=True)  46.1 us
    all_to_all x1, waiting for transfers between devices, shards(): lax.all_to_all(partial_out, 'req', split_axis=0, concat_axis=0, tiled=True)  24.6 us
    all_to_all x1, blocking collectives, shards(): both = lax.all_to_all(both, 'tp', split_axis=0, concat_axis=0, tiled=True)  22.2 us
    all_to_all x1, starting transfers between devices, shards(): lax.all_to_all(partial_out, 'req', split_axis=0, concat_axis=0, tiled=True)  6.25 us
    all_to_all x1, starting transfers between devices, shards(): lax.all_to_all(jnp.broadcast_to(proj_part[None], (tp_count,) + proj_part....  4.01 us
    pallas_call x1, Pallas kernels, local_attention(): pl.pallas_call(attention_kernel, out_shape=jax.ShapeDtypeStruct((row_coun...  3.95 us
    all_to_all x1, waiting for transfers between devices, shards(): lax.all_to_all(jnp.broadcast_to(proj_part[None], (tp_count,) + proj_part....  3.34 us
  transfers between devices with their start and end apart: 2, of which 2 were waited for; matrix products, arithmetic and copies ran while one was open for 2% of the time, Pallas kernels for 0%

profile of v10, /device:TPU:33, one launch (start us, length us, event | category | flops | bytes accessed | tf_op | source)
XLA Modules:
  0.0 119.1 jit_solution(3587718588087994386)
XLA Ops:
  0.0 0.0 copy-start
  0.0 0.0 copy-start.1
  0.0 0.0 copy-start.4
  0.0 3.9 %shard_map.136 = f32[4,2304]{1,0:T(4,128)} custom-call(s32[4]{0:T(128)} %len_ref.1, bf16[4,576]{1,0:T(4,128)(2,1)} %q_ref.1, bf16[4,576]{1,0:T(4,128)(2,1)} %nk_ref.1, bf16[4,576]{1,0:T(4,128)(2,1)} %nv_ref.1, bf16[4,576,128]{2,1,0:T(8,128)(2,1)} %bitcast.20, bf16[4,576,128]{2,1,0:T(8,128)(2,1)} %bitcast.21, bf16[576,2304]{1,0:T(8,128)(2,1)} %w_hbm.1), custom_call_target="tpu_custom_call" | custom-call | flops 10616832 | bytes 3852288 | tf_op jit(solution)/shard_map/pallas_call | solution.py:86
  4.0 0.0 copy-start.2
  4.0 0.0 copy-start.3
  4.0 1.5 %broadcast_in_dim.18 = f32[4,4,2304]{2,1,0:T(4,128)} broadcast(f32[4,2304]{1,0:T(4,128)} %shard_map.136), dimensions={1,2} | broadcast | bytes 184320 | tf_op jit(solution)/shard_map/broadcast_in_dim | solution.py:151
  5.5 4.0 %all-to-all-start = ((f32[4,4,2304]{2,1,0:T(4,128)}), f32[4,4,2304]{2,1,0:T(4,128)S(1)}, u32[]{:S(2)}, u32[]{:S(2)}) async-start(f32[4,4,2304]{2,1,0:T(4,128)} %broadcast_in_dim.18), calls=%async_computation | async-start | bytes 294912 | tf_op jit(solution)/shard_map/all_to_all | solution.py:150
  9.5 0.7 constant_dynamic-slice_fusion.1
  10.3 0.1 copy.38
  10.4 0.1 iota_compare_fusion.1
  10.4 0.1 eq.65
  10.5 0.1 fusion.14
  10.6 0.2 select_reduce_fusion
  10.8 0.1 eq.69
  10.9 0.1 copy.39
  11.0 0.1 and_reduce_fusion
  11.1 3.3 %all-to-all-done = f32[4,4,2304]{2,1,0:T(4,128)S(1)} async-done(((f32[4,4,2304]{2,1,0:T(4,128)}), f32[4,4,2304]{2,1,0:T(4,128)S(1)}, u32[]{:S(2)}, u32[]{:S(2)}) %all-to-all-start) | async-done | bytes 147488 | tf_op jit(solution)/shard_map/all_to_all | solution.py:150
  14.5 0.0 copy-done.1
  14.5 0.1 multiply_reduce_fusion
  14.6 0.0 copy-done.4
  14.6 0.2 convolution_convert_fusion.2
  14.9 0.2 broadcast_in_dim.21
  15.1 46.1 %all_to_all.20 = bf16[128,2,576]{2,1,0:T(2,128)(2,1)S(1)} all-to-all(bf16[128,2,576]{2,1,0:T(2,128)(2,1)S(1)} %bitcast.19), channel_id=1, replica_groups=mesh['req'=128,'tp'=4] {'req'}, dimensions={0} | all-to-all | bytes 589824 | tf_op jit(solution)/shard_map/all_to_all | solution.py:173
  61.2 0.2 reshape.160
  61.4 0.0 copy-done.2
  61.4 0.0 copy-done.3
  61.4 0.9 convolution_convert_fusion
  62.4 0.1 broadcast_in_dim.22
  62.5 22.2 %all_to_all.21 = bf16[4,256,720]{1,2,0:T(8,128)(2,1)S(1)} all-to-all(bf16[4,256,720]{1,2,0:T(8,128)(2,1)S(1)} %broadcast_in_dim.22), channel_id=1, replica_groups=mesh['req'=128,'tp'=4] {'tp'}, dimensions={0} | all-to-all | bytes 2949120 | tf_op jit(solution)/shard_map/all_to_all | solution.py:180
  84.7 0.2 convert_reduce_fusion
  84.9 0.0 copy-done
  84.9 0.4 convolution_convert_fusion.1
  85.3 0.2 copy.41
  85.5 0.9 reshape.161
  86.4 6.2 %all-to-all-start.3 = ((bf16[128,2,576]{2,1,0:T(2,128)(2,1)}), bf16[128,2,576]{2,1,0:T(2,128)(2,1)S(1)}, u32[]{:S(2)}, u32[]{:S(2)}) async-start(bf16[128,2,576]{2,1,0:T(2,128)(2,1)} %reshape.161), calls=%async_computation.3 | async-start | bytes 655360 | tf_op jit(solution)/shard_map/all_to_all | solution.py:189
  92.6 0.8 constant_dynamic-slice_fusion
  93.4 0.1 fusion.9
  93.5 24.6 %all-to-all-done.3 = bf16[128,2,576]{2,1,0:T(2,128)(2,1)S(1)} async-done(((bf16[128,2,576]{2,1,0:T(2,128)(2,1)}), bf16[128,2,576]{2,1,0:T(2,128)(2,1)S(1)}, u32[]{:S(2)}, u32[]{:S(2)}) %all-to-all-start.3) | async-done | bytes 294944 | tf_op jit(solution)/shard_map/all_to_all | solution.py:189
  118.0 0.3 convert_reduce_fusion.1
  118.3 0.8 fusion.1
  (5 shorter events, 0.1 us)
Async XLA Ops:
  0.0 84.9 %copy-start = (bf16[360,576]{0,1:T(8,128)(2,1)S(1)}, bf16[360,576]{0,1:T(8,128)(2,1)}, u32[]{:S(2)}) copy-start(bf16[360,576]{0,1:T(8,128)(2,1)} %param.27) | copy-start | bytes 1244164
  0.0 14.5 %copy-start.1 = (bf16[4,2304]{1,0:T(4,128)(2,1)S(1)}, bf16[4,2304]{1,0:T(4,128)(2,1)}, u32[]{:S(2)}) copy-start(bf16[4,2304]{1,0:T(4,128)(2,1)} %param.20) | copy-start | bytes 55300
  0.0 14.6 %copy-start.4 = (f32[576]{0:T(1024)S(1)}, f32[576]{0:T(1024)}, u32[]{:S(2)}) copy-start(f32[576]{0:T(1024)} %param.22) | copy-start | bytes 6916
  4.0 57.5 %copy-start.2 = (bf16[576,360]{1,0:T(8,128)(2,1)S(1)}, bf16[576,360]{1,0:T(8,128)(2,1)}, u32[]{:S(2)}) copy-start(bf16[576,360]{1,0:T(8,128)(2,1)} %param.26) | copy-start | bytes 1244164
  4.0 57.5 %copy-start.3 = (bf16[576,360]{1,0:T(8,128)(2,1)S(1)}, bf16[576,360]{1,0:T(8,128)(2,1)}, u32[]{:S(2)}) copy-start(bf16[576,360]{1,0:T(8,128)(2,1)} %param.25) | copy-start | bytes 1244164
  5.5 8.9 %all-to-all-start = ((f32[4,4,2304]{2,1,0:T(4,128)}), f32[4,4,2304]{2,1,0:T(4,128)S(1)}, u32[]{:S(2)}, u32[]{:S(2)}) async-start(f32[4,4,2304]{2,1,0:T(4,128)} %broadcast_in_dim.18), calls=%async_computation | async-start | bytes 294912 | tf_op jit(solution)/shard_map/all_to_all | solution.py:150
  86.4 31.7 %all-to-all-start.3 = ((bf16[128,2,576]{2,1,0:T(2,128)(2,1)}), bf16[128,2,576]{2,1,0:T(2,128)(2,1)S(1)}, u32[]{:S(2)}, u32[]{:S(2)}) async-start(bf16[128,2,576]{2,1,0:T(2,128)(2,1)} %reshape.161), calls=%async_computation.3 | async-start | bytes 655360 | tf_op jit(solution)/shard_map/all_to_all | solution.py:189

commit v11 on v10

--- a/solution.py
+++ b/solution.py
@@ -172,15 +172,28 @@
     outgoing = jnp.repeat(expert_rows, group_size, axis=0)
     arrived = lax.all_to_all(outgoing, "req", split_axis=0, concat_axis=0, tiled=True)
     token_rows = arrived.reshape(req_count * capacity, share)
-    paired_weight = jnp.concatenate([gate_weight, up_weight], axis=1)
-    both = jnp.dot(token_rows, paired_weight, preferred_element_type=jnp.float32).astype(
-        jnp.bfloat16
-    )
-    both = jnp.broadcast_to(both[None], (tp_count,) + both.shape)
+    chunk = gate_weight.shape[1] // tp_count
+    paired_weight = jnp.concatenate(
+        [
+            gate_weight.reshape(share, tp_count, chunk),
+            up_weight.reshape(share, tp_count, chunk),
+        ],
+        axis=2,
+    )
+    both = jnp.einsum(
+        "sf,ftk->tsk", token_rows, paired_weight, preferred_element_type=jnp.float32
+    ).astype(jnp.bfloat16)
     both = lax.all_to_all(both, "tp", split_axis=0, concat_axis=0, tiled=True)
     summed = jnp.sum(both.astype(jnp.float32), axis=0)
-    hidden_units = gate_weight.shape[1]
-    activ = (jax.nn.silu(summed[:, :hidden_units]) * summed[:, hidden_units:]).astype(jnp.bfloat16)
+    activ_chunk = (jax.nn.silu(summed[:, :chunk]) * summed[:, chunk:]).astype(jnp.bfloat16)
+    activ_all = lax.all_to_all(
+        jnp.broadcast_to(activ_chunk[None], (tp_count,) + activ_chunk.shape),
+        "tp",
+        split_axis=0,
+        concat_axis=0,
+        tiled=True,
+    )
+    activ = jnp.moveaxis(activ_all, 0, 1).reshape(activ_chunk.shape[0], tp_count * chunk)
     partial_out = (
         jnp.dot(activ, down_weight, preferred_element_type=jnp.float32)
         .astype(jnp.bfloat16)

time: 120 us -> 117 us (0.975)
  blocking collectives: 68.3 us -> 17.6 us
  waiting for transfers between devices: 27.9 us -> 52.5 us
  starting transfers between devices: 10.3 us -> 32.6 us
  local copies, waits for them, and re-layouts: 5 us -> 6.44 us
    all_to_all x1, blocking collectives: 46.1 us -> 7.54 us  [shards(): lax.all_to_all(jnp.broadcast_to(activ_chunk[None], (tp_count,) + activ_ch...]
    all_to_all x0 -> x1, waiting for transfers between devices: none -> 24.6 us  [shards(): lax.all_to_all(outgoing, 'req', split_axis=0, concat_axis=0, tiled=True)]
    all_to_all x0 -> x1, starting transfers between devices: none -> 20.9 us  [shards(): lax.all_to_all(outgoing, 'req', split_axis=0, concat_axis=0, tiled=True)]
    all_to_all x1, blocking collectives: 22.2 us -> 10.1 us  [shards(): both = lax.all_to_all(both, 'tp', split_axis=0, concat_axis=0, tiled=True)]
    all_to_all x1, starting transfers between devices: 6.25 us -> 7.7 us  [shards(): lax.all_to_all(partial_out, 'req', split_axis=0, concat_axis=0, tiled=True)]
  transfers between devices with their start and end apart: 2 -> 3, of which waited for: 2 -> 3; matrix products, arithmetic and copies ran while one was open for 2% -> 3% of each run, Pallas kernels for 0% -> 0%
where the time goes in v11:
time: 117 us; the launch traced here: 116 us
  waiting for transfers between devices  52.5 us (45%)
  starting transfers between devices  32.6 us (28%)
  blocking collectives  17.6 us (15%)
  local copies, waits for them, and re-layouts  6.44 us (6%)
  Pallas kernels  3.95 us (3%)
  matrix products  1.86 us (2%)
    all_to_all x1, waiting for transfers between devices, shards(): lax.all_to_all(outgoing, 'req', split_axis=0, concat_axis=0, tiled=True)  24.6 us
    all_to_all x1, waiting for transfers between devices, shards(): lax.all_to_all(partial_out, 'req', split_axis=0, concat_axis=0, tiled=True)  24.6 us
    all_to_all x1, starting transfers between devices, shards(): lax.all_to_all(outgoing, 'req', split_axis=0, concat_axis=0, tiled=True)  20.9 us
    all_to_all x1, blocking collectives, shards(): both = lax.all_to_all(both, 'tp', split_axis=0, concat_axis=0, tiled=True)  10.1 us
    all_to_all x1, starting transfers between devices, shards(): lax.all_to_all(partial_out, 'req', split_axis=0, concat_axis=0, tiled=True)  7.7 us
    all_to_all x1, blocking collectives, shards(): lax.all_to_all(jnp.broadcast_to(activ_chunk[None], (tp_count,) + activ_ch...  7.54 us
    all_to_all x1, starting transfers between devices, shards(): lax.all_to_all(jnp.broadcast_to(proj_part[None], (tp_count,) + proj_part....  4.01 us
    pallas_call x1, Pallas kernels, local_attention(): pl.pallas_call(attention_kernel, out_shape=jax.ShapeDtypeStruct((row_coun...  3.95 us
  transfers between devices with their start and end apart: 3, of which 3 were waited for; matrix products, arithmetic and copies ran while one was open for 3% of the time, Pallas kernels for 0%

profile of v11, /device:TPU:33, one launch (start us, length us, event | category | flops | bytes accessed | tf_op | source)
XLA Modules:
  0.0 116.3 jit_solution(1975338524380866863)
XLA Ops:
  0.0 0.0 copy-start
  0.0 0.0 copy-start.3
  0.0 0.0 copy-start.4
  0.0 3.9 %shard_map.136 = f32[4,2304]{1,0:T(4,128)} custom-call(s32[4]{0:T(128)} %len_ref.1, bf16[4,576]{1,0:T(4,128)(2,1)} %q_ref.1, bf16[4,576]{1,0:T(4,128)(2,1)} %nk_ref.1, bf16[4,576]{1,0:T(4,128)(2,1)} %nv_ref.1, bf16[4,576,128]{2,1,0:T(8,128)(2,1)} %bitcast.32, bf16[4,576,128]{2,1,0:T(8,128)(2,1)} %bitcast.33, bf16[576,2304]{1,0:T(8,128)(2,1)} %w_hbm.1), custom_call_target="tpu_custom_call" | custom-call | flops 10616832 | bytes 3852288 | tf_op jit(solution)/shard_map/pallas_call | solution.py:86
  4.0 0.0 copy-start.1
  4.0 0.0 copy-start.2
  4.0 1.5 %broadcast_in_dim.18 = f32[4,4,2304]{2,1,0:T(4,128)} broadcast(f32[4,2304]{1,0:T(4,128)} %shard_map.136), dimensions={1,2} | broadcast | bytes 184320 | tf_op jit(solution)/shard_map/broadcast_in_dim | solution.py:151
  5.5 4.0 %all-to-all-start = ((f32[4,4,2304]{2,1,0:T(4,128)}), f32[4,4,2304]{2,1,0:T(4,128)S(1)}, u32[]{:S(2)}, u32[]{:S(2)}) async-start(f32[4,4,2304]{2,1,0:T(4,128)} %broadcast_in_dim.18), calls=%async_computation | async-start | bytes 294912 | tf_op jit(solution)/shard_map/all_to_all | solution.py:150
  9.5 0.7 constant_dynamic-slice_fusion.1
  10.3 0.1 copy.38
  10.4 0.1 iota_compare_fusion.1
  10.4 0.1 eq.65
  10.5 0.1 fusion.14
  10.6 0.2 select_reduce_fusion
  10.8 0.1 eq.69
  10.9 0.1 copy.39
  11.0 0.1 and_reduce_fusion
  11.1 3.3 %all-to-all-done = f32[4,4,2304]{2,1,0:T(4,128)S(1)} async-done(((f32[4,4,2304]{2,1,0:T(4,128)}), f32[4,4,2304]{2,1,0:T(4,128)S(1)}, u32[]{:S(2)}, u32[]{:S(2)}) %all-to-all-start) | async-done | bytes 147488 | tf_op jit(solution)/shard_map/all_to_all | solution.py:150
  14.5 0.0 copy-done.3
  14.5 0.1 multiply_reduce_fusion
  14.6 0.0 copy-done.4
  14.6 0.2 convolution_convert_fusion.2
  14.9 0.9 broadcast_in_dim.21
  15.8 20.9 %all-to-all-start.1 = ((bf16[128,2,576]{2,1,0:T(2,128)(2,1)}), bf16[128,2,576]{2,1,0:T(2,128)(2,1)S(1)}, u32[]{:S(2)}, u32[]{:S(2)}) async-start(bf16[128,2,576]{2,1,0:T(2,128)(2,1)} %bitcast.3), calls=%async_computation.1 | async-start | bytes 655360 | tf_op jit(solution)/shard_map/all_to_all | solution.py:173
  36.7 0.0 copy-done.1
  36.7 0.2 copy.41
  36.9 0.1 reshape.169
  37.1 0.0 copy-done.2
  37.1 0.2 copy.40
  37.3 0.1 reshape.168
  37.5 24.6 %all-to-all-done.1 = bf16[128,2,576]{2,1,0:T(2,128)(2,1)S(1)} async-done(((bf16[128,2,576]{2,1,0:T(2,128)(2,1)}), bf16[128,2,576]{2,1,0:T(2,128)(2,1)S(1)}, u32[]{:S(2)}, u32[]{:S(2)}) %all-to-all-start.1) | async-done | bytes 294944 | tf_op jit(solution)/shard_map/all_to_all | solution.py:173
  62.1 0.2 reshape.171
  62.3 0.5 fusion
  62.8 10.1 %all_to_all.25 = bf16[4,256,180]{1,2,0:T(8,128)(2,1)S(1)} all-to-all(bf16[4,256,180]{1,2,0:T(8,128)(2,1)S(1)} %fusion), channel_id=1, replica_groups=mesh['req'=128,'tp'=4] {'tp'}, dimensions={0} | all-to-all | bytes 737280 | tf_op jit(solution)/shard_map/all_to_all | solution.py:186
  73.1 7.5 %all_to_all.26 = bf16[4,256,90]{1,2,0:T(8,128)(2,1)S(1)} all-to-all(bf16[4,256,90]{1,2,0:T(8,128)(2,1)S(1)} %broadcast_in_dim.22), channel_id=1, replica_groups=mesh['req'=128,'tp'=4] {'tp'}, dimensions={0} | all-to-all | bytes 368640 | tf_op jit(solution)/shard_map/all_to_all | solution.py:189
  80.6 0.1 reshape.172
  80.7 0.0 copy-done
  80.7 0.3 convolution_convert_fusion.1
  81.0 0.2 copy.44
  81.2 0.9 reshape.173
  82.0 7.7 %all-to-all-start.4 = ((bf16[128,2,576]{2,1,0:T(2,128)(2,1)}), bf16[128,2,576]{2,1,0:T(2,128)(2,1)S(1)}, u32[]{:S(2)}, u32[]{:S(2)}) async-start(bf16[128,2,576]{2,1,0:T(2,128)(2,1)} %reshape.173), calls=%async_computation.4 | async-start | bytes 655360 | tf_op jit(solution)/shard_map/all_to_all | solution.py:202
  89.7 0.8 constant_dynamic-slice_fusion
  90.5 0.1 fusion.9
  90.6 24.6 %all-to-all-done.4 = bf16[128,2,576]{2,1,0:T(2,128)(2,1)S(1)} async-done(((bf16[128,2,576]{2,1,0:T(2,128)(2,1)}), bf16[128,2,576]{2,1,0:T(2,128)(2,1)S(1)}, u32[]{:S(2)}, u32[]{:S(2)}) %all-to-all-start.4) | async-done | bytes 294944 | tf_op jit(solution)/shard_map/all_to_all | solution.py:202
  115.1 0.3 convert_reduce_fusion.1
  115.4 0.8 fusion.2
  (8 shorter events, 0.2 us)
Async XLA Ops:
  0.0 80.7 %copy-start = (bf16[360,576]{0,1:T(8,128)(2,1)S(1)}, bf16[360,576]{0,1:T(8,128)(2,1)}, u32[]{:S(2)}) copy-start(bf16[360,576]{0,1:T(8,128)(2,1)} %param.27) | copy-start | bytes 1244164
  0.0 14.5 %copy-start.3 = (bf16[4,2304]{1,0:T(4,128)(2,1)S(1)}, bf16[4,2304]{1,0:T(4,128)(2,1)}, u32[]{:S(2)}) copy-start(bf16[4,2304]{1,0:T(4,128)(2,1)} %param.20) | copy-start | bytes 55300
  0.0 14.6 %copy-start.4 = (f32[576]{0:T(1024)S(1)}, f32[576]{0:T(1024)}, u32[]{:S(2)}) copy-start(f32[576]{0:T(1024)} %param.22) | copy-start | bytes 6916
  4.0 32.7 %copy-start.1 = (bf16[576,360]{1,0:T(8,128)(2,1)S(1)}, bf16[576,360]{1,0:T(8,128)(2,1)}, u32[]{:S(2)}) copy-start(bf16[576,360]{1,0:T(8,128)(2,1)} %param.26) | copy-start | bytes 1244164
  4.0 33.1 %copy-start.2 = (bf16[576,360]{1,0:T(8,128)(2,1)S(1)}, bf16[576,360]{1,0:T(8,128)(2,1)}, u32[]{:S(2)}) copy-start(bf16[576,360]{1,0:T(8,128)(2,1)} %param.25) | copy-start | bytes 1244164
  5.5 8.9 %all-to-all-start = ((f32[4,4,2304]{2,1,0:T(4,128)}), f32[4,4,2304]{2,1,0:T(4,128)S(1)}, u32[]{:S(2)}, u32[]{:S(2)}) async-start(f32[4,4,2304]{2,1,0:T(4,128)} %broadcast_in_dim.18), calls=%async_computation | async-start | bytes 294912 | tf_op jit(solution)/shard_map/all_to_all | solution.py:150
  15.8 46.3 %all-to-all-start.1 = ((bf16[128,2,576]{2,1,0:T(2,128)(2,1)}), bf16[128,2,576]{2,1,0:T(2,128)(2,1)S(1)}, u32[]{:S(2)}, u32[]{:S(2)}) async-start(bf16[128,2,576]{2,1,0:T(2,128)(2,1)} %bitcast.3), calls=%async_computation.1 | async-start | bytes 655360 | tf_op jit(solution)/shard_map/all_to_all | solution.py:173
  82.0 33.1 %all-to-all-start.4 = ((bf16[128,2,576]{2,1,0:T(2,128)(2,1)}), bf16[128,2,576]{2,1,0:T(2,128)(2,1)S(1)}, u32[]{:S(2)}, u32[]{:S(2)}) async-start(bf16[128,2,576]{2,1,0:T(2,128)(2,1)} %reshape.173), calls=%async_computation.4 | async-start | bytes 655360 | tf_op jit(solution)/shard_map/all_to_all | solution.py:202

commit v12 on v11

--- a/solution.py
+++ b/solution.py
@@ -76,16 +76,17 @@
             preferred_element_type=jnp.float32,
         )
         total = part if total is None else total + part
-    o_ref[...] = total
-
-
-def local_attention(query, new_key, new_value, key_cache, value_cache, lengths, out_weight):
+    for copy_index in range(o_ref.shape[0]):
+        o_ref[copy_index] = total
+
+
+def local_attention(query, new_key, new_value, key_cache, value_cache, lengths, out_weight, copies):
     row_count, local_width = query.shape
     cache_len = key_cache.shape[1]
     vmem = pl.BlockSpec(memory_space=pltpu.VMEM)
     return pl.pallas_call(
         attention_kernel,
-        out_shape=jax.ShapeDtypeStruct((row_count, out_weight.shape[1]), jnp.float32),
+        out_shape=jax.ShapeDtypeStruct((copies, row_count, out_weight.shape[1]), jnp.float32),
         in_specs=[pl.BlockSpec(memory_space=pltpu.SMEM)] + [vmem] * 5 + [pl.BlockSpec(memory_space=pl.ANY)],
         out_specs=vmem,
         scratch_shapes=[
@@ -139,16 +140,16 @@
     down_weight,
 ):
     row_count = query.shape[0]
-    proj_part = local_attention(
-        query, new_key, new_value, key_cache, value_cache, lengths, out_weight
+    tp_count = lax.axis_size("tp")
+    proj_copies = local_attention(
+        query, new_key, new_value, key_cache, value_cache, lengths, out_weight, tp_count
     )
     model_width = out_weight.shape[1]
     share = model_width // lax.axis_size("tp")
     col_start = lax.axis_index("tp") * share
     resid_float = resid.astype(jnp.float32)
-    tp_count = lax.axis_size("tp")
     proj_all = lax.all_to_all(
-        jnp.broadcast_to(proj_part[None], (tp_count,) + proj_part.shape),
+        proj_copies,
         "tp",
         split_axis=0,
         concat_axis=0,

time: 117 us -> 115 us (0.983)
  local copies, waits for them, and re-layouts: 6.44 us -> 4.94 us
    broadcast_in_dim x1 -> x0, local copies, waits for them, and re-layouts: 1.52 us -> none  [shards(): jnp.broadcast_to(proj_part[None], (tp_count,) + proj_part.shape)]
where the time goes in v12:
time: 115 us
  waiting for transfers between devices  52.5 us (46%)
  starting transfers between devices  32.8 us (29%)
  blocking collectives  17.6 us (15%)
  local copies, waits for them, and re-layouts  4.94 us (4%)
  Pallas kernels  4.02 us (3%)
  matrix products  1.86 us (2%)
    all_to_all x1, waiting for transfers between devices, shards(): lax.all_to_all(outgoing, 'req', split_axis=0, concat_axis=0, tiled=True)  24.6 us
    all_to_all x1, waiting for transfers between devices, shards(): lax.all_to_all(partial_out, 'req', split_axis=0, concat_axis=0, tiled=True)  24.6 us
    all_to_all x1, starting transfers between devices, shards(): lax.all_to_all(outgoing, 'req', split_axis=0, concat_axis=0, tiled=True)  20.9 us
    all_to_all x1, blocking collectives, shards(): both = lax.all_to_all(both, 'tp', split_axis=0, concat_axis=0, tiled=True)  10.1 us
    all_to_all x1, starting transfers between devices, shards(): lax.all_to_all(partial_out, 'req', split_axis=0, concat_axis=0, tiled=True)  7.69 us
    all_to_all x1, blocking collectives, shards(): lax.all_to_all(jnp.broadcast_to(activ_chunk[None], (tp_count,) + activ_ch...  7.54 us
    all_to_all x1, starting transfers between devices, shards(): lax.all_to_all(proj_copies, 'tp', split_axis=0, concat_axis=0, tiled=True)  4.16 us
    pallas_call x1, Pallas kernels, local_attention(): pl.pallas_call(attention_kernel, out_shape=jax.ShapeDtypeStruct((copies,...  4.02 us
  transfers between devices with their start and end apart: 3, of which 3 were waited for; matrix products, arithmetic and copies ran while one was open for 3% of the time, Pallas kernels for 0%

profile of v12, /device:TPU:33, one launch (start us, length us, event | category | flops | bytes accessed | tf_op | source)
XLA Modules:
  0.0 115.0 jit_solution(10138650985839994322)
XLA Ops:
  0.0 0.0 copy-start
  0.0 0.0 copy-start.3
  0.0 0.0 copy-start.4
  0.0 0.0 copy-start.1
  0.0 4.0 %shard_map.136 = f32[4,4,2304]{2,1,0:T(4,128)} custom-call(s32[4]{0:T(128)} %len_ref.1, bf16[4,576]{1,0:T(4,128)(2,1)} %q_ref.1, bf16[4,576]{1,0:T(4,128)(2,1)} %nk_ref.1, bf16[4,576]{1,0:T(4,128)(2,1)} %nv_ref.1, bf16[4,576,128]{2,1,0:T(8,128)(2,1)} %bitcast.32, bf16[4,576,128]{2,1,0:T(8,128)(2,1)} %bitcast.33, bf16[576,2304]{1,0:T(8,128)(2,1)} %w_hbm.1), custom_call_target="tpu_custom_call" | custom-call | flops 10616832 | bytes 3852288 | tf_op jit(solution)/shard_map/pallas_call | solution.py:87
  4.0 0.0 copy-start.2
  4.1 4.2 %all-to-all-start = ((f32[4,4,2304]{2,1,0:T(4,128)}), f32[4,4,2304]{2,1,0:T(4,128)S(1)}, u32[]{:S(2)}, u32[]{:S(2)}) async-start(f32[4,4,2304]{2,1,0:T(4,128)} %shard_map.136), calls=%async_computation | async-start | bytes 294912 | tf_op jit(solution)/shard_map/all_to_all | solution.py:151
  8.2 0.7 constant_dynamic-slice_fusion.1
  9.0 0.1 copy.38
  9.1 0.1 iota_compare_fusion.1
  9.1 0.1 eq.65
  9.2 0.1 fusion.14
  9.3 0.2 select_reduce_fusion
  9.5 0.1 eq.69
  9.6 0.1 copy.39
  9.7 0.1 and_reduce_fusion
  9.8 3.3 %all-to-all-done = f32[4,4,2304]{2,1,0:T(4,128)S(1)} async-done(((f32[4,4,2304]{2,1,0:T(4,128)}), f32[4,4,2304]{2,1,0:T(4,128)S(1)}, u32[]{:S(2)}, u32[]{:S(2)}) %all-to-all-start) | async-done | bytes 147488 | tf_op jit(solution)/shard_map/all_to_all | solution.py:151
  13.2 0.0 copy-done.3
  13.2 0.1 multiply_reduce_fusion
  13.3 0.0 copy-done.4
  13.3 0.2 convolution_convert_fusion.2
  13.6 0.9 broadcast_in_dim.18
  14.5 20.9 %all-to-all-start.1 = ((bf16[128,2,576]{2,1,0:T(2,128)(2,1)}), bf16[128,2,576]{2,1,0:T(2,128)(2,1)S(1)}, u32[]{:S(2)}, u32[]{:S(2)}) async-start(bf16[128,2,576]{2,1,0:T(2,128)(2,1)} %bitcast.3), calls=%async_computation.1 | async-start | bytes 655360 | tf_op jit(solution)/shard_map/all_to_all | solution.py:174
  35.4 0.0 copy-done.1
  35.4 0.3 copy.41
  35.6 0.1 reshape.168
  35.8 0.0 copy-done.2
  35.8 0.3 copy.40
  36.1 0.1 reshape.167
  36.2 24.6 %all-to-all-done.1 = bf16[128,2,576]{2,1,0:T(2,128)(2,1)S(1)} async-done(((bf16[128,2,576]{2,1,0:T(2,128)(2,1)}), bf16[128,2,576]{2,1,0:T(2,128)(2,1)S(1)}, u32[]{:S(2)}, u32[]{:S(2)}) %all-to-all-start.1) | async-done | bytes 294944 | tf_op jit(solution)/shard_map/all_to_all | solution.py:174
  60.8 0.2 reshape.170
  61.0 0.5 fusion
  61.5 10.1 %all_to_all.25 = bf16[4,256,180]{1,2,0:T(8,128)(2,1)S(1)} all-to-all(bf16[4,256,180]{1,2,0:T(8,128)(2,1)S(1)} %fusion), channel_id=1, replica_groups=mesh['req'=128,'tp'=4] {'tp'}, dimensions={0} | all-to-all | bytes 737280 | tf_op jit(solution)/shard_map/all_to_all | solution.py:187
  71.8 7.5 %all_to_all.26 = bf16[4,256,90]{1,2,0:T(8,128)(2,1)S(1)} all-to-all(bf16[4,256,90]{1,2,0:T(8,128)(2,1)S(1)} %broadcast_in_dim.30), channel_id=1, replica_groups=mesh['req'=128,'tp'=4] {'tp'}, dimensions={0} | all-to-all | bytes 368640 | tf_op jit(solution)/shard_map/all_to_all | solution.py:190
  79.3 0.1 reshape.171
  79.4 0.0 copy-done
  79.4 0.3 convolution_convert_fusion.1
  79.7 0.2 copy.44
  79.9 0.9 reshape.172
  80.7 7.7 %all-to-all-start.4 = ((bf16[128,2,576]{2,1,0:T(2,128)(2,1)}), bf16[128,2,576]{2,1,0:T(2,128)(2,1)S(1)}, u32[]{:S(2)}, u32[]{:S(2)}) async-start(bf16[128,2,576]{2,1,0:T(2,128)(2,1)} %reshape.172), calls=%async_computation.4 | async-start | bytes 655360 | tf_op jit(solution)/shard_map/all_to_all | solution.py:203
  88.4 0.8 constant_dynamic-slice_fusion
  89.2 0.1 fusion.9
  89.3 24.6 %all-to-all-done.4 = bf16[128,2,576]{2,1,0:T(2,128)(2,1)S(1)} async-done(((bf16[128,2,576]{2,1,0:T(2,128)(2,1)}), bf16[128,2,576]{2,1,0:T(2,128)(2,1)S(1)}, u32[]{:S(2)}, u32[]{:S(2)}) %all-to-all-start.4) | async-done | bytes 294944 | tf_op jit(solution)/shard_map/all_to_all | solution.py:203
  113.8 0.3 convert_reduce_fusion.1
  114.1 0.8 fusion.2
  (8 shorter events, 0.2 us)
Async XLA Ops:
  0.0 79.4 %copy-start = (bf16[360,576]{0,1:T(8,128)(2,1)S(1)}, bf16[360,576]{0,1:T(8,128)(2,1)}, u32[]{:S(2)}) copy-start(bf16[360,576]{0,1:T(8,128)(2,1)} %param.27) | copy-start | bytes 1244164
  0.0 13.2 %copy-start.3 = (bf16[4,2304]{1,0:T(4,128)(2,1)S(1)}, bf16[4,2304]{1,0:T(4,128)(2,1)}, u32[]{:S(2)}) copy-start(bf16[4,2304]{1,0:T(4,128)(2,1)} %param.20) | copy-start | bytes 55300
  0.0 13.3 %copy-start.4 = (f32[576]{0:T(1024)S(1)}, f32[576]{0:T(1024)}, u32[]{:S(2)}) copy-start(f32[576]{0:T(1024)} %param.22) | copy-start | bytes 6916
  0.0 35.4 %copy-start.1 = (bf16[576,360]{1,0:T(8,128)(2,1)S(1)}, bf16[576,360]{1,0:T(8,128)(2,1)}, u32[]{:S(2)}) copy-start(bf16[576,360]{1,0:T(8,128)(2,1)} %param.26) | copy-start | bytes 1244164
  4.0 31.7 %copy-start.2 = (bf16[576,360]{1,0:T(8,128)(2,1)S(1)}, bf16[576,360]{1,0:T(8,128)(2,1)}, u32[]{:S(2)}) copy-start(bf16[576,360]{1,0:T(8,128)(2,1)} %param.25) | copy-start | bytes 1244164
  4.1 9.1 %all-to-all-start = ((f32[4,4,2304]{2,1,0:T(4,128)}), f32[4,4,2304]{2,1,0:T(4,128)S(1)}, u32[]{:S(2)}, u32[]{:S(2)}) async-start(f32[4,4,2304]{2,1,0:T(4,128)} %shard_map.136), calls=%async_computation | async-start | bytes 294912 | tf_op jit(solution)/shard_map/all_to_all | solution.py:151
  14.5 46.3 %all-to-all-start.1 = ((bf16[128,2,576]{2,1,0:T(2,128)(2,1)}), bf16[128,2,576]{2,1,0:T(2,128)(2,1)S(1)}, u32[]{:S(2)}, u32[]{:S(2)}) async-start(bf16[128,2,576]{2,1,0:T(2,128)(2,1)} %bitcast.3), calls=%async_computation.1 | async-start | bytes 655360 | tf_op jit(solution)/shard_map/all_to_all | solution.py:174
  80.7 33.1 %all-to-all-start.4 = ((bf16[128,2,576]{2,1,0:T(2,128)(2,1)}), bf16[128,2,576]{2,1,0:T(2,128)(2,1)S(1)}, u32[]{:S(2)}, u32[]{:S(2)}) async-start(bf16[128,2,576]{2,1,0:T(2,128)(2,1)} %reshape.172), calls=%async_computation.4 | async-start | bytes 655360 | tf_op jit(solution)/shard_map/all_to_all | solution.py:203
